TPU v7x, 32 devices: a whole 2x2x4 slice. The times are simulated.
32 devices in a mesh: ctx: 8 (over z, y), tp: 4 (over x, core).
Axes of the slice: x: 2, y: 2, z: 4, core: 2. Of those that a mesh axis runs over, the one named last changes fastest.
Arguments:
- tokens: bfloat16 [6144, 4096], P('ctx'), may hold values from -6 to 6
- in_weight: bfloat16 [4096, 3, 4096], P('ctx', None, 'tp'), may hold values from -0.09375 to 0.09375
- short_taps: float32 [3, 4096, 7], P(None, 'tp'), may hold values from -2.5 to 2.5
- medium_taps: float32 [4096, 128], P('tp'), may hold values from -2 to 2
- medium_decay: float32 [4096], P('tp'), may hold values from 0.01 to 0.3
- skip_gain: float32 [4096], P('tp'), may hold values from 0.5 to 1.5
- out_weight: bfloat16 [4096, 4096], P('tp'), may hold values from -0.09375 to 0.09375
Outputs:
- mixed: bfloat16 [6144, 4096], P('ctx', 'tp')
All inputs are finite; a program needn't handle non-finite values.
Results may differ from a plain program's by a relative error of at most 0.0072.
Values may be sent and summed in bfloat16 or wider, within the bound.
No kernel may reach another device: no remote copies, remote signals or barrier semaphores. Data moves between devices by JAX's collectives and lax.ppermute only.
A program may use at most 192 MiB of HBM per device.

v0:
```python
import jax
import jax.numpy as jnp
from jax import lax
from jax.sharding import PartitionSpec as P


def skewed(extended):
    group_size = extended.shape[0]
    width = extended.shape[1] // 2
    reverse = extended[:, ::-1]
    tiled = jnp.tile(reverse, (1, width))
    flat = tiled[:, width - 1 : width - 1 + width * (2 * width - 1)]
    return flat.reshape(group_size, width, 2 * width - 1)[:, :, :width]


def toeplitz_pair(filters):
    blank = jnp.zeros(filters.shape, jnp.float32)
    lower = skewed(jnp.concatenate([blank, filters], axis=1))
    upper = skewed(jnp.concatenate([filters, blank], axis=1))
    return (lower, upper)


def channel_filter(fields, short_weights, filters, skip_weights):
    group_size = fields.shape[1]
    length = fields.shape[2]
    short_count = short_weights.shape[2]
    medium_count = filters.shape[1]
    widened = jnp.pad(fields.astype(jnp.float32), ((0, 0), (0, 0), (short_count - 1, 0)))
    smoothed = jnp.zeros(fields.shape, jnp.float32)
    for lag_step in range(short_count):
        start_col = short_count - 1 - lag_step
        smoothed = (
            smoothed
            + short_weights[:, :, lag_step : lag_step + 1]
            * widened[:, :, start_col : start_col + length]
        )
    product = smoothed[1] * smoothed[2]
    blocks = product.reshape(group_size, -1, medium_count)
    earlier = jnp.concatenate(
        [jnp.zeros((group_size, 1, medium_count), jnp.float32), blocks[:, :-1]], axis=1
    )
    lower, upper = toeplitz_pair(filters)
    response = jnp.einsum("cbj,cij->cbi", blocks, lower, precision=lax.Precision.HIGHEST)
    response = response + jnp.einsum(
        "cbj,cij->cbi", earlier, upper, precision=lax.Precision.HIGHEST
    )
    response = response.reshape(group_size, -1)
    return (smoothed[0] * (response + skip_weights[:, None] * product)).astype(jnp.bfloat16)


def per_device(tokens, in_weight, short_taps, medium_taps, medium_decay, skip_gain, out_weight):
    row_count = tokens.shape[0]
    channel_count = in_weight.shape[2]
    ctx_count = lax.axis_size("ctx")
    group_size = channel_count // ctx_count
    medium_count = medium_taps.shape[1]
    features = jnp.einsum(
        "rd,dkc->rkc",
        tokens,
        lax.all_gather(in_weight, "ctx", axis=0, tiled=True),
        preferred_element_type=jnp.float32,
    ).astype(jnp.bfloat16)
    lag_values = lax.broadcasted_iota(jnp.float32, (1, medium_count), 1)
    filters = medium_taps * jnp.exp(-medium_decay[:, None] * lag_values)
    tilted = jnp.transpose(features, (1, 2, 0))
    spread = lax.all_to_all(tilted, "ctx", split_axis=1, concat_axis=2, tiled=True)
    offset = lax.axis_index("ctx") * group_size
    short_local = lax.dynamic_slice_in_dim(short_taps, offset, group_size, 1)
    filter_local = lax.dynamic_slice_in_dim(filters, offset, group_size, 0)
    skip_local = lax.dynamic_slice_in_dim(skip_gain, offset, group_size, 0)
    filtered = channel_filter(spread, short_local, filter_local, skip_local)
    filtered = filtered.reshape(group_size, ctx_count, row_count)
    returned = lax.all_to_all(filtered, "ctx", split_axis=1, concat_axis=0, tiled=True)
    gated = returned.reshape(channel_count, row_count)
    summed = lax.psum_scatter(
        lax.dot_general(
            out_weight, gated, (((0,), (0,)), ((), ())), preferred_element_type=jnp.float32
        ),
        "tp",
        scatter_dimension=0,
        tiled=True,
    )
    return jnp.transpose(summed).astype(jnp.bfloat16)


def solution(mesh):
    return jax.shard_map(
        per_device,
        mesh=mesh,
        in_specs=(
            P("ctx", None),
            P("ctx", None, "tp"),
            P(None, "tp", None),
            P("tp", None),
            P("tp"),
            P("tp"),
            P("tp", None),
        ),
        out_specs=P("ctx", "tp"),
        check_vma=False,
    )
```

profile of v0, /device:TPU:1, one launch (start us, length us, event | category | flops | bytes accessed | tf_op | source)
XLA Modules:
  0.0 935.1 jit_solution(1060447155559455234)
XLA Ops:
  6.5 0.0 all-gather.2.cloned.1.call-start
  6.5 4.7 copy.21
  11.2 0.0 all-gather.2.cloned.1.call-update
  11.3 482.7 %all-gather.2.cloned.1.call-done = bf16[4096,3,1024]{0,2,1:T(8,128)(2,1)} async-done(((bf16[512,3,1024]{0,2,1:T(8,128)(2,1)}), bf16[4096,3,1024]{0,2,1:T(8,128)(2,1)}) %all-gather.2.cloned.1.call-update) | async-done | bytes 25165840 | tf_op jit(solution)/shard_map/all_gather | solution.py:60
  493.9 24.9 %fusion.9 = bf16[3,1024,768]{2,1,0:T(8,128)(2,1)S(1)} fusion(bf16[4096,3,1024]{0,2,1:T(8,128)(2,1)} %all-gather.2.cloned.1.call-done, bf16[768,4096]{1,0:T(8,128)(2,1)} %param.7), kind=kOutput, calls=%fused_computation.14 | convolution fusion | flops 19329712128 | bytes 36175872 | tf_op jit(solution)/shard_map/rd,dkc->rkc/dot_general | solution.py:57
  518.9 6.6 copy.22
  525.5 0.0 copy-start.2
  525.5 4.9 all-to-all-start
  530.4 0.0 reduce-scatter.2.cloned.1.call-start
  530.4 0.0 copy-done.2
  530.4 0.8 dynamic_slice.11
  531.2 0.1 dynamic-slice.7
  531.3 1.0 constant_dynamic-slice_fusion.5
  532.3 0.9 dynamic-slice_multiply_fusion
  533.3 0.4 rev.6
  533.7 0.2 rev.7
  533.9 1.3 tile.20
  535.2 20.7 %copy.38 = f32[16,8,128,256]{3,1,2,0:T(8,128)S(1)} copy(f32[16,8,128,256]{3,2,1,0:T(8,128)S(1)} %bitcast.46) | data formatting | bytes 33554432
  555.9 7.5 slice.91
  563.3 28.9 %reshape.44 = f32[128,128,255]{2,1,0:T(8,128)} reshape(f32[128,32640]{1,0:T(8,128)} %slice.91) | data formatting | bytes 33423360 | tf_op jit(solution)/shard_map/reshape | solution.py:13
  592.2 1.3 tile.8
  593.6 20.7 %copy.37 = f32[16,8,128,256]{3,1,2,0:T(8,128)S(1)} copy(f32[16,8,128,256]{3,2,1,0:T(8,128)S(1)} %bitcast.47) | data formatting | bytes 33554432
  614.2 7.6 slice.88
  621.8 28.9 %reshape.43 = f32[128,128,255]{2,1,0:T(8,128)} reshape(f32[128,32640]{1,0:T(8,128)} %slice.88) | data formatting | bytes 33423360 | tf_op jit(solution)/shard_map/reshape | solution.py:13
  650.7 17.2 %all-to-all-done = bf16[3,1024,768]{2,0,1:T(4,128)(2,1)} async-done(((bf16[3,1024,768]{2,0,1:T(4,128)(2,1)}), bf16[3,1024,768]{2,0,1:T(4,128)(2,1)}, u32[]{:S(2)}, u32[]{:S(2)}) %all-to-all-start) | async-done | bytes 4718624 | tf_op jit(solution)/shard_map/all_to_all | solution.py:66
  667.9 3.4 copy.23
  671.4 4.8 convert_bitcast_fusion
  676.1 9.6 %copy.24 = f32[3,128,8,768]{1,3,2,0:T(8,128)} copy(f32[3,128,8,768]{3,1,2,0:T(8,128)} %convert_bitcast_fusion) | data formatting | bytes 18874368 | tf_op jit(solution)/shard_map/convert_element_type | solution.py:28
  685.7 30.6 %multiply_add_fusion = f32[3,128,6144]{1,2,0:T(8,128)} fusion(f32[3,128,6144]{1,2,0:T(8,128)} %bitcast.50, f32[3,128]{1,0:T(4,128)S(1)} %get-tuple-element.16, f32[3,128]{1,0:T(4,128)S(1)} %get-tuple-element.17, f32[3,128]{1,0:T(4,128)S(1)} %get-tuple-element.18, f32[3,128]{1,0:T(4,128)S(1)} %get-tuple-element.19, f32[3,128]{1,0:T(4,128)S(1)} %get-tuple-element.20, ...), kind=kLoop, calls=%fused_computation.1 | loop fusion | flops 30670848 | bytes 18885120 | tf_op jit(solution)/shard_map/add | solution.py:33
  716.3 5.9 slice_multiply_fusion
  722.2 3.5 copy.28
  725.7 2.4 copy.29
  728.1 2.3 copy.26
  730.5 0.0 copy-start
  730.5 16.0 %fusion = f32[128,48,128]{2,1,0:T(8,128)S(1)} fusion(f32[128,128,255]{2,1,0:T(8,128)} %reshape.44, f32[128,47,128]{2,1,0:T(8,128)} %bitcast.53), kind=kOutput, calls=%fused_computation.2 | convolution fusion | flops 1207959552 | bytes 14680064 | tf_op jit(solution)/shard_map/cbj,cij->cbi/dot_general | solution.py:44
  746.5 0.0 copy-done
  746.5 0.0 copy-start.1
  746.5 17.1 %fusion.12 = f32[128,48,128]{2,1,0:T(8,128)} fusion(f32[128,48,128]{2,1,0:T(8,128)S(1)} %fusion, f32[128,48,128]{2,1,0:T(8,128)S(1)} %copy-done, f32[128,128,255]{2,1,0:T(8,128)} %reshape.43), kind=kOutput, calls=%fused_computation.15 | convolution fusion | flops 1208745984 | bytes 17825792 | tf_op jit(solution)/shard_map/cbj,cij->cbi/dot_general | solution.py:43
  763.6 4.6 reshape.45
  768.3 0.0 copy-done.1
  768.3 4.1 fusion.7
  772.4 40.1 %all_to_all.24 = bf16[128,8,768]{2,0,1:T(8,128)(2,1)S(1)} all-to-all(bf16[128,8,768]{2,0,1:T(8,128)(2,1)S(1)} %fusion.7), channel_id=1, replica_groups=mesh['ctx'=8,'tp'=4] {'ctx'}, dimensions={1} | all-to-all | bytes 3145728 | tf_op jit(solution)/shard_map/all_to_all | solution.py:73
  812.5 12.5 %convolution_bitcast_fusion = f32[4096,768]{0,1:T(8,128)} fusion(bf16[1024,768]{1,0:T(8,128)(2,1)S(1)} %bitcast.56, bf16[1024,4096]{1,0:T(8,128)(2,1)} %param.13), kind=kOutput, calls=%fused_computation.6 | convolution fusion | flops 6442450944 | bytes 22544384 | tf_op jit(solution)/shard_map/dot_general | solution.py:76
  825.0 0.0 reduce-scatter.2.cloned.1.call-update
  825.0 99.5 %reduce-scatter.2.cloned.1.call-done = f32[1024,768]{0,1:T(8,128)} async-done(((f32[4096,768]{0,1:T(8,128)}), f32[1024,768]{0,1:T(8,128)}) %reduce-scatter.2.cloned.1.call-update) | async-done | bytes 3145744 | tf_op jit(solution)/shard_map/reduce_scatter | solution.py:75
  924.5 3.3 convert_bitcast_fusion.1
  (6 shorter events, 0.0 us)
Async XLA Ops:
  6.5 487.4 %all-gather.2.cloned.1.call-start = ((), (), s32[]{:S(2)}) async-start(), calls=%async_computation.3 | async-start | bytes 28311552 | tf_op jit(solution)/shard_map/all_gather | solution.py:60
  525.5 4.9 copy-start.2
  525.5 142.4 %all-to-all-start = ((bf16[3,1024,768]{2,0,1:T(4,128)(2,1)}), bf16[3,1024,768]{2,0,1:T(4,128)(2,1)}, u32[]{:S(2)}, u32[]{:S(2)}) async-start(bf16[3,1024,768]{2,0,1:T(4,128)(2,1)} %copy.22), calls=%async_computation | async-start | bytes 12582912 | tf_op jit(solution)/shard_map/all_to_all | solution.py:66
  530.4 394.2 %reduce-scatter.2.cloned.1.call-start = ((), (), s32[]{:S(2)}) async-start(), calls=%async_computation.4 | async-start | bytes 15728640 | tf_op jit(solution)/shard_map/reduce_scatter | solution.py:75
  730.5 16.0 %copy-start = (f32[128,48,128]{2,1,0:T(8,128)S(1)}, f32[128,48,128]{2,1,0:T(8,128)}, u32[]{:S(2)}) copy-start(f32[128,48,128]{2,1,0:T(8,128)} %copy.29) | copy-start | bytes 9437188
  746.5 21.8 %copy-start.1 = (f32[128,8,768]{2,0,1:T(8,128)S(1)}, f32[128,8,768]{2,0,1:T(8,128)}, u32[]{:S(2)}) copy-start(f32[128,8,768]{2,0,1:T(8,128)} %copy.28) | copy-start | bytes 9437188
Sparse Core Ops, SparseCore 0:
  11.4 482.5 all-gather.1
  825.1 99.3 reduce-scatter.1
where the time goes:
time: 943 us; the launch traced here: 935 us
  waiting for transfers between devices  599 us (64%)
  local copies, waits for them, and re-layouts  156 us (17%)
  matrix products  70.6 us (7%)
  other arithmetic  49.6 us (5%)
  blocking collectives  40.1 us (4%)
  between operations  14 us (1%)
    all_gather x1, waiting for transfers between devices, per_device(): lax.all_gather(in_weight, 'ctx', axis=0, tiled=True)  483 us
    reduce_scatter x1, waiting for transfers between devices, per_device(): lax.psum_scatter(lax.dot_general(out_weight, gated, (((0,), (0,)), ((), (...  99.5 us
    reshape x2, local copies, waits for them, and re-layouts, skewed(): return flat.reshape(group_size, width, 2 * width - 1)[:, :, :width]  57.8 us
    unnamed x13, local copies, waits for them, and re-layouts  46.1 us
    all_to_all x1, blocking collectives, per_device(): lax.all_to_all(filtered, 'ctx', split_axis=1, concat_axis=0, tiled=True)  40.1 us
    add x1, other arithmetic, channel_filter(): smoothed + short_weights[:, :, lag_step:lag_step + 1] * widened[:, :, sta...  30.6 us
    dot_general x1, matrix products, per_device(): jnp.einsum('rd,dkc->rkc', tokens, lax.all_gather(in_weight, 'ctx', axis=0...  24.9 us
  transfers between devices with their start and end apart: 3, of which 3 were waited for; matrix products, arithmetic and copies ran while one was open for 13% of the time, Pallas kernels for 0%

commit v1 on v0

--- a/solution.py
+++ b/solution.py
@@ -48,18 +48,77 @@
     return (smoothed[0] * (response + skip_weights[:, None] * product)).astype(jnp.bfloat16)
 
 
+def ring_order(count):
+    if count % 2:
+        return list(range(count))
+    return list(range(0, count, 2)) + list(range(count - 1, 0, -2))
+
+
+def ring_projection(tokens, in_weight):
+    count = lax.axis_size("ctx")
+    rows = in_weight.shape[0]
+    order = ring_order(count)
+    place = [0] * count
+    for at, member in enumerate(order):
+        place[member] = at
+    forward = [(order[k], order[(k + 1) % count]) for k in range(count)]
+    backward = [(order[k], order[(k - 1) % count]) for k in range(count)]
+    me = lax.axis_index("ctx")
+    order_table = jnp.array(order, jnp.int32)
+    my_place = jnp.array(place, jnp.int32)[me]
+
+    def partial(block, source, start, width):
+        cols = lax.dynamic_slice_in_dim(tokens, source * rows + start, width, 1)
+        return jnp.einsum("rd,dkc->rkc", cols, block, preferred_element_type=jnp.float32)
+
+    total = partial(in_weight, me, 0, rows)
+    full_steps = (count - 1) // 2
+    half = rows // 2
+
+    def sources(step):
+        return (
+            order_table[(my_place - step) % count],
+            order_table[(my_place + step) % count],
+        )
+
+    def add_pair(total, ahead, behind, step):
+        from_behind, from_ahead = sources(step)
+        total = total + partial(ahead, from_behind, 0, rows)
+        return total + partial(behind, from_ahead, 0, rows)
+
+    def ring_step(step, carry):
+        ahead, behind, total = carry
+        moved_ahead = lax.ppermute(ahead, "ctx", forward)
+        moved_behind = lax.ppermute(behind, "ctx", backward)
+        total = add_pair(total, ahead, behind, step - 1)
+        return (moved_ahead, moved_behind, total)
+
+    if full_steps == 0:
+        return total
+    ahead = lax.ppermute(in_weight, "ctx", forward)
+    behind = lax.ppermute(in_weight, "ctx", backward)
+    ahead, behind, total = lax.fori_loop(
+        2, full_steps + 1, ring_step, (ahead, behind, total)
+    )
+    if count % 2 == 0:
+        last_ahead = lax.ppermute(ahead[:half], "ctx", forward)
+        last_behind = lax.ppermute(behind[half:], "ctx", backward)
+        total = add_pair(total, ahead, behind, full_steps)
+        from_behind, from_ahead = sources(full_steps + 1)
+        total = total + partial(last_ahead, from_behind, 0, half)
+        total = total + partial(last_behind, from_ahead, half, rows - half)
+    else:
+        total = add_pair(total, ahead, behind, full_steps)
+    return total
+
+
 def per_device(tokens, in_weight, short_taps, medium_taps, medium_decay, skip_gain, out_weight):
     row_count = tokens.shape[0]
     channel_count = in_weight.shape[2]
     ctx_count = lax.axis_size("ctx")
     group_size = channel_count // ctx_count
     medium_count = medium_taps.shape[1]
-    features = jnp.einsum(
-        "rd,dkc->rkc",
-        tokens,
-        lax.all_gather(in_weight, "ctx", axis=0, tiled=True),
-        preferred_element_type=jnp.float32,
-    ).astype(jnp.bfloat16)
+    features = ring_projection(tokens, in_weight).astype(jnp.bfloat16)
     lag_values = lax.broadcasted_iota(jnp.float32, (1, medium_count), 1)
     filters = medium_taps * jnp.exp(-medium_decay[:, None] * lag_values)
     tilted = jnp.transpose(features, (1, 2, 0))

time: 943 us -> 711 us (0.75)
  waiting for transfers between devices: 599 us -> 284 us
  matrix products: 70.6 us -> 115 us
  local copies, waits for them, and re-layouts: 156 us -> 174 us
    all_gather x1 -> x0, waiting for transfers between devices: 483 us -> none  [per_device(): lax.all_gather(in_weight, 'ctx', axis=0, tiled=True)]
    ppermute x0 -> x8, waiting for transfers between devices: none -> 173 us  [the longest x2 100 us: ring_step(): moved_ahead = lax.ppermute(ahead, 'ctx', forward)]
    dot_general x1 -> x9, matrix products: 24.9 us -> 69.3 us  [partial(): jnp.einsum('rd,dkc->rkc', cols, block, preferred_element_type=jnp.float32)]
    while x0 -> x12, local copies, waits for them, and re-layouts: none -> 11.5 us
    transpose x0 -> x1, local copies, waits for them, and re-layouts: none -> 10.4 us  [per_device(): tilted = jnp.transpose(features, (1, 2, 0))]
    unnamed x13 -> x14, local copies, waits for them, and re-layouts: 46.1 us -> 41.4 us
  transfers between devices with their start and end apart: 3 -> 10, of which waited for: 3 -> 10; matrix products, arithmetic and copies ran while one was open for 13% -> 26% of each run, Pallas kernels for 0% -> 0%
where the time goes in v1:
time: 711 us; the launch traced here: 703 us
  waiting for transfers between devices  284 us (40%)
  local copies, waits for them, and re-layouts  174 us (24%)
  matrix products  115 us (16%)
  other arithmetic  49.6 us (7%)
  blocking collectives  45 us (6%)
  between operations  18.8 us (3%)
  starting transfers between devices  12 us (2%)
    ppermute x2, waiting for transfers between devices, ring_step(): moved_ahead = lax.ppermute(ahead, 'ctx', forward)  100 us
    reduce_scatter x1, waiting for transfers between devices, per_device(): lax.psum_scatter(lax.dot_general(out_weight, gated, (((0,), (0,)), ((), (...  99.5 us
    dot_general x9, matrix products, partial(): jnp.einsum('rd,dkc->rkc', cols, block, preferred_element_type=jnp.float32)  69.3 us
    ppermute x1, waiting for transfers between devices, ring_projection(): ahead = lax.ppermute(in_weight, 'ctx', forward)  58.4 us
    reshape x2, local copies, waits for them, and re-layouts, skewed(): return flat.reshape(group_size, width, 2 * width - 1)[:, :, :width]  57.8 us
    all_to_all x1, blocking collectives, per_device(): lax.all_to_all(filtered, 'ctx', split_axis=1, concat_axis=0, tiled=True)  45 us
    unnamed x14, local copies, waits for them, and re-layouts  41.4 us
    add x1, other arithmetic, channel_filter(): smoothed + short_weights[:, :, lag_step:lag_step + 1] * widened[:, :, sta...  30.6 us
  transfers between devices with their start and end apart: 10, of which 10 were waited for; matrix products, arithmetic and copies ran while one was open for 26% of the time, Pallas kernels for 0%

profile of v1, /device:TPU:1, one launch (start us, length us, event | category | flops | bytes accessed | tf_op | source)
XLA Modules:
  0.0 702.9 jit_solution(17499293496093764278)
XLA Ops:
  6.5 2.1 collective-permute-start.2
  9.9 8.5 %fusion.22 = f32[768,3,1024]{2,0,1:T(8,128)} fusion(bf16[512,3,1024]{2,0,1:T(8,128)(2,1)} %param.12, bf16[768,4096]{1,0:T(8,128)(2,1)} %param.11, s32[]{:T(128)S(6)} %select_n.141), kind=kOutput, calls=%fused_computation.28 | convolution fusion | flops 2415919104 | bytes 13369348 | tf_op jit(solution)/shard_map/rd,dkc->rkc/dot_general | solution.py:72
  18.4 58.4 %collective-permute-done.2 = bf16[512,3,1024]{2,0,1:T(8,128)(2,1)} collective-permute-done((bf16[512,3,1024]{2,0,1:T(8,128)(2,1)}, bf16[512,3,1024]{2,0,1:T(8,128)(2,1)}, u32[]{:S(2)}, u32[]{:S(2)}) %collective-permute-start.2) | collective-permute-done | bytes 3145760 | tf_op jit(solution)/shard_map/ppermute | solution.py:98
  77.6 148.0 %while.22 = (s32[]{:T(128)}, bf16[512,3,1024]{2,0,1:T(8,128)(2,1)}, bf16[512,3,1024]{2,0,1:T(8,128)(2,1)}, f32[768,3,1024]{2,0,1:T(8,128)}, s32[]{:T(128)}, /*in...) while((s32[]{:T(128)}, bf16[512,3,1024]{2,0,1:T(8,128)(2,1)}, ...), condition=%wide.region_1.2_spmd.clone, body=%wide.region_0.1_spmd.sunk.clone.sunk | while | flops 4836556800 | bytes 158859952 | solution.py:100
  77.6 3.8 copy.55
  82.8 1.9 copy.56
  87.8 4.9 fusion.66
  92.7 6.0 add_add_fusion.2
  98.8 50.7 %collective-permute-done = bf16[512,3,1024]{2,0,1:T(8,128)(2,1)} collective-permute-done((bf16[512,3,1024]{2,0,1:T(8,128)(2,1)}, bf16[512,3,1024]{2,0,1:T(8,128)(2,1)}, u32[]{:S(2)}, u32[]{:S(2)}) %collective-permute-start) | collective-permute-done | bytes 3145760 | tf_op jit(solution)/shard_map/while/body/eval_jaxpr/ppermute | solution.py:91
  149.5 2.7 collective-permute-done.1
  152.2 3.8 copy.55
  157.3 1.9 copy.56
  162.4 4.9 fusion.66
  167.3 6.0 add_add_fusion.2
  173.4 49.5 %collective-permute-done = bf16[512,3,1024]{2,0,1:T(8,128)(2,1)} collective-permute-done((bf16[512,3,1024]{2,0,1:T(8,128)(2,1)}, bf16[512,3,1024]{2,0,1:T(8,128)(2,1)}, u32[]{:S(2)}, u32[]{:S(2)}) %collective-permute-start) | collective-permute-done | bytes 3145760 | tf_op jit(solution)/shard_map/while/body/eval_jaxpr/ppermute | solution.py:91
  222.9 2.7 collective-permute-done.1
  233.9 1.5 slice.72
  236.1 8.4 %fusion.18 = f32[768,3,1024]{2,0,1:T(8,128)} fusion(bf16[512,3,1024]{2,0,1:T(8,128)(2,1)} %get-tuple-element.239, bf16[768,4096]{1,0:T(8,128)(2,1)} %get-tuple-element.382, s32[]{:T(128)S(6)} %select_n.148), kind=kOutput, calls=%fused_computation.24 | convolution fusion | flops 2415919104 | bytes 13369348 | tf_op jit(solution)/shard_map/rd,dkc->rkc/dot_general | solution.py:72
  244.6 8.4 %fusion.20 = f32[768,3,1024]{2,0,1:T(8,128)} fusion(bf16[512,3,1024]{2,0,1:T(8,128)(2,1)} %get-tuple-element.238, bf16[768,4096]{1,0:T(8,128)(2,1)} %get-tuple-element.382, s32[]{:T(128)S(6)} %select_n.145), kind=kOutput, calls=%fused_computation.26 | convolution fusion | flops 2415919104 | bytes 13369348 | tf_op jit(solution)/shard_map/rd,dkc->rkc/dot_general | solution.py:72
  253.0 5.9 collective-permute-done.4
  258.9 6.6 fusion.31
  265.5 1.7 collective-permute-done.5
  267.3 15.6 %fusion.11 = bf16[3,1024,768]{1,2,0:T(8,128)(2,1)} fusion(f32[768,3,1024]{2,0,1:T(8,128)} %fusion.31, f32[768,3,1024]{2,0,1:T(8,128)} %fusion.18, f32[768,3,1024]{2,0,1:T(8,128)} %get-tuple-element.237, f32[768,3,1024]{2,0,1:T(8,128)} %fusion.20, bf16[256,3,1024]{2,0,1:T(8,128)(2,1)S(1)} %collective-permute-done.5, ...), kind=kOutput, calls=%fused_computation.16 | convolution fusion | flops 1219756032 | bytes 44433412 | tf_op jit(solution)/shard_map/rd,dkc->rkc/dot_general | solution.py:72
  282.8 10.4 %copy.20 = bf16[3,1024,768]{2,0,1:T(4,128)(2,1)} copy(bf16[3,1024,768]{1,2,0:T(8,128)(2,1)} %fusion.11) | data formatting | bytes 9437184 | tf_op jit(solution)/shard_map/transpose | solution.py:124
  293.2 4.9 all-to-all-start
  303.1 20.7 %copy.36 = f32[16,8,128,256]{3,1,2,0:T(8,128)S(1)} copy(f32[16,8,128,256]{3,2,1,0:T(8,128)S(1)} %bitcast.92) | data formatting | bytes 33554432
  323.8 7.5 %slice.99 = f32[128,32640]{1,0:T(8,128)} slice(f32[128,32768]{1,0:T(8,128)S(1)} %bitcast.94), slice={[0:128], [127:32767]} | slice | bytes 33423360 | tf_op jit(solution)/shard_map/slice | solution.py:12
  331.3 28.9 %reshape.60 = f32[128,128,255]{2,1,0:T(8,128)} reshape(f32[128,32640]{1,0:T(8,128)} %slice.99) | data formatting | bytes 33423360 | tf_op jit(solution)/shard_map/reshape | solution.py:13
  361.5 20.7 %copy.35 = f32[16,8,128,256]{3,1,2,0:T(8,128)S(1)} copy(f32[16,8,128,256]{3,2,1,0:T(8,128)S(1)} %bitcast.93) | data formatting | bytes 33554432
  382.2 7.6 %slice.96 = f32[128,32640]{1,0:T(8,128)} slice(f32[128,32768]{1,0:T(8,128)S(1)} %bitcast.95), slice={[0:128], [127:32767]} | slice | bytes 33423360 | tf_op jit(solution)/shard_map/slice | solution.py:12
  389.8 28.9 %reshape.59 = f32[128,128,255]{2,1,0:T(8,128)} reshape(f32[128,32640]{1,0:T(8,128)} %slice.96) | data formatting | bytes 33423360 | tf_op jit(solution)/shard_map/reshape | solution.py:13
  418.7 12.1 %all-to-all-done = bf16[3,1024,768]{2,0,1:T(4,128)(2,1)} async-done(((bf16[3,1024,768]{2,0,1:T(4,128)(2,1)}), bf16[3,1024,768]{2,0,1:T(4,128)(2,1)}, u32[]{:S(2)}, u32[]{:S(2)}) %all-to-all-start) | async-done | bytes 4718624 | tf_op jit(solution)/shard_map/all_to_all | solution.py:125
  430.8 3.4 copy.21
  434.2 4.8 convert_bitcast_fusion
  439.0 9.6 %copy.22 = f32[3,128,8,768]{1,3,2,0:T(8,128)} copy(f32[3,128,8,768]{3,1,2,0:T(8,128)} %convert_bitcast_fusion) | data formatting | bytes 18874368 | tf_op jit(solution)/shard_map/convert_element_type | solution.py:28
  448.6 30.6 %multiply_add_fusion = f32[3,128,6144]{1,2,0:T(8,128)} fusion(f32[3,128,6144]{1,2,0:T(8,128)} %bitcast.96, f32[3,128]{1,0:T(4,128)S(1)} %get-tuple-element.290, f32[3,128]{1,0:T(4,128)S(1)} %get-tuple-element.291, f32[3,128]{1,0:T(4,128)S(1)} %get-tuple-element.292, f32[3,128]{1,0:T(4,128)S(1)} %get-tuple-element.293, f32[3,128]{1,0:T(4,128)S(1)} %get-tuple-element.294, ...), kind=kLoop, calls=%fused_computation.9 | loop fusion | flops 30670848 | bytes 18885120 | tf_op jit(solution)/shard_map/add | solution.py:33
  479.2 5.9 slice_multiply_fusion
  485.1 3.5 copy.26
  488.7 2.4 copy.27
  491.0 2.4 copy.24
  493.4 16.0 %fusion.7 = f32[128,48,128]{2,1,0:T(8,128)S(1)} fusion(f32[128,128,255]{2,1,0:T(8,128)} %reshape.60, f32[128,47,128]{2,1,0:T(8,128)} %bitcast.99), kind=kOutput, calls=%fused_computation.11 | convolution fusion | flops 1207959552 | bytes 14680064 | tf_op jit(solution)/shard_map/cbj,cij->cbi/dot_general | solution.py:44
  509.4 17.0 %fusion.15 = f32[128,48,128]{2,1,0:T(8,128)} fusion(f32[128,48,128]{2,1,0:T(8,128)S(1)} %fusion.7, f32[128,48,128]{2,1,0:T(8,128)S(1)} %copy-done.2, f32[128,128,255]{2,1,0:T(8,128)} %reshape.59), kind=kOutput, calls=%fused_computation.22 | convolution fusion | flops 1208745984 | bytes 17825792 | tf_op jit(solution)/shard_map/cbj,cij->cbi/dot_general | solution.py:43
  526.4 4.8 reshape.61
  531.2 4.1 fusion.13
  535.3 45.0 %all_to_all.24 = bf16[128,8,768]{2,0,1:T(8,128)(2,1)S(1)} all-to-all(bf16[128,8,768]{2,0,1:T(8,128)(2,1)S(1)} %fusion.13), channel_id=1, replica_groups=mesh['ctx'=8,'tp'=4] {'ctx'}, dimensions={1} | all-to-all | bytes 3145728 | tf_op jit(solution)/shard_map/all_to_all | solution.py:132
  580.2 12.5 %convolution_bitcast_fusion = f32[4096,768]{0,1:T(8,128)} fusion(bf16[1024,768]{1,0:T(8,128)(2,1)S(1)} %bitcast.102, bf16[1024,4096]{1,0:T(8,128)(2,1)} %param.17), kind=kOutput, calls=%fused_computation.15 | convolution fusion | flops 6442450944 | bytes 22544384 | tf_op jit(solution)/shard_map/dot_general | solution.py:135
  592.8 99.5 %reduce-scatter.2.cloned.1.call-done = f32[1024,768]{0,1:T(8,128)} async-done(((f32[4096,768]{0,1:T(8,128)}), f32[1024,768]{0,1:T(8,128)}) %reduce-scatter.2.cloned.1.call-update) | async-done | bytes 3145744 | tf_op jit(solution)/shard_map/reduce_scatter | solution.py:134
  692.4 3.3 convert_bitcast_fusion.1
  (45 shorter events, 16.8 us)
Async XLA Ops:
  6.5 70.2 %collective-permute-start.2 = (bf16[512,3,1024]{2,0,1:T(8,128)(2,1)}, bf16[512,3,1024]{2,0,1:T(8,128)(2,1)}, u32[]{:S(2)}, u32[]{:S(2)}) collective-permute-start(bf16[512,3,1024]{2,0,1:T(8,128)(2,1)} %param.12), channel_id=1, source_target_pairs={{0,8},{8,16},{16,24},{24,28},{28,20},{20,12},{12,4},{4,0},{1,9},{9... | collective-permute-start | bytes 9437192 | tf_op jit(solution)/shard_map/ppermute | solution.py:98
  8.7 69.0 %collective-permute-start.3 = (bf16[512,3,1024]{2,0,1:T(8,128)(2,1)}, bf16[512,3,1024]{2,0,1:T(8,128)(2,1)}, u32[]{:S(2)}, u32[]{:S(2)}) collective-permute-start(bf16[512,3,1024]{2,0,1:T(8,128)(2,1)} %param.12), channel_id=1, source_target_pairs={{0,4},{8,0},{16,8},{24,16},{28,24},{20,28},{12,20},{4,12},{1,5},{9... | collective-permute-start | bytes 9437192 | tf_op jit(solution)/shard_map/ppermute | solution.py:99
  9.9 67.7 %copy-start.4 = (s32[8]{0:T(128)S(1)}, s32[8]{0:T(128)}, u32[]{:S(2)}) copy-start(s32[8]{0:T(128)} %constant.163.clone) | copy-start | bytes 100
  81.5 68.0 %collective-permute-start = (bf16[512,3,1024]{2,0,1:T(8,128)(2,1)}, bf16[512,3,1024]{2,0,1:T(8,128)(2,1)}, u32[]{:S(2)}, u32[]{:S(2)}) collective-permute-start(bf16[512,3,1024]{2,0,1:T(8,128)(2,1)} %copy.55), channel_id=1, source_target_pairs={{0,8},{8,16},{16,24},{24,28},{28,20},{20,12},{12,4},{4,0},{1,9},{9... | collective-permute-start | bytes 9437192 | tf_op jit(solution)/shard_map/while/body/eval_jaxpr/ppermute | solution.py:91
  84.7 67.6 %collective-permute-start.1 = (bf16[512,3,1024]{2,0,1:T(8,128)(2,1)S(1)}, bf16[512,3,1024]{2,0,1:T(8,128)(2,1)}, u32[]{:S(2)}, u32[]{:S(2)}) collective-permute-start(bf16[512,3,1024]{2,0,1:T(8,128)(2,1)S(1)} %copy.56), channel_id=1, source_target_pairs={{0,4},{8,0},{16,8},{24,16},{28,24},{20,28},{12,20},{4,12},{1,5},{9... | collective-permute-start | bytes 9437192 | tf_op jit(solution)/shard_map/while/body/eval_jaxpr/ppermute | solution.py:92
  87.8 4.9 copy-start
  98.8 53.4 %copy-start.1 = (f32[768,3,1024]{2,0,1:T(8,128)}, f32[768,3,1024]{2,0,1:T(8,128)S(1)}, u32[]{:S(2)}) copy-start(f32[768,3,1024]{2,0,1:T(8,128)S(1)} %add_add_fusion.2) | copy-start | bytes 28311556 | tf_op jit(solution)/shard_map/while
  156.0 66.8 %collective-permute-start = (bf16[512,3,1024]{2,0,1:T(8,128)(2,1)}, bf16[512,3,1024]{2,0,1:T(8,128)(2,1)}, u32[]{:S(2)}, u32[]{:S(2)}) collective-permute-start(bf16[512,3,1024]{2,0,1:T(8,128)(2,1)} %copy.55), channel_id=1, source_target_pairs={{0,8},{8,16},{16,24},{24,28},{28,20},{20,12},{12,4},{4,0},{1,9},{9... | collective-permute-start | bytes 9437192 | tf_op jit(solution)/shard_map/while/body/eval_jaxpr/ppermute | solution.py:91
  159.2 66.4 %collective-permute-start.1 = (bf16[512,3,1024]{2,0,1:T(8,128)(2,1)S(1)}, bf16[512,3,1024]{2,0,1:T(8,128)(2,1)}, u32[]{:S(2)}, u32[]{:S(2)}) collective-permute-start(bf16[512,3,1024]{2,0,1:T(8,128)(2,1)S(1)} %copy.56), channel_id=1, source_target_pairs={{0,4},{8,0},{16,8},{24,16},{28,24},{20,28},{12,20},{4,12},{1,5},{9... | collective-permute-start | bytes 9437192 | tf_op jit(solution)/shard_map/while/body/eval_jaxpr/ppermute | solution.py:92
  162.4 4.9 copy-start
  173.4 52.2 %copy-start.1 = (f32[768,3,1024]{2,0,1:T(8,128)}, f32[768,3,1024]{2,0,1:T(8,128)S(1)}, u32[]{:S(2)}) copy-start(f32[768,3,1024]{2,0,1:T(8,128)S(1)} %add_add_fusion.2) | copy-start | bytes 28311556 | tf_op jit(solution)/shard_map/while
  227.1 31.8 %collective-permute-start.4 = (bf16[256,3,1024]{2,0,1:T(8,128)(2,1)S(1)}, bf16[256,3,1024]{2,0,1:T(8,128)(2,1)}, u32[]{:S(2)}, u32[]{:S(2)}) collective-permute-start(bf16[256,3,1024]{2,0,1:T(8,128)(2,1)S(1)} %slice.71), channel_id=1, source_target_pairs={{0,8},{8,16},{16,24},{24,28},{28,20},{20,12},{12,4},{4,0},{1,9},{9... | collective-permute-start | bytes 4718600 | tf_op jit(solution)/shard_map/ppermute | solution.py:104
  235.4 31.9 %collective-permute-start.5 = (bf16[256,3,1024]{2,0,1:T(8,128)(2,1)S(1)}, bf16[256,3,1024]{2,0,1:T(8,128)(2,1)S(1)}, u32[]{:S(2)}, u32[]{:S(2)}) collective-permute-start(bf16[256,3,1024]{2,0,1:T(8,128)(2,1)S(1)} %slice.72), channel_id=1, source_target_pairs={{0,4},{8,0},{16,8},{24,16},{28,24},{20,28},{12,20},{4,12},{1,5},{9... | collective-permute-start | bytes 4718600 | tf_op jit(solution)/shard_map/ppermute | solution.py:105
  293.2 5.0 copy-start.5
  293.2 137.6 %all-to-all-start = ((bf16[3,1024,768]{2,0,1:T(4,128)(2,1)}), bf16[3,1024,768]{2,0,1:T(4,128)(2,1)}, u32[]{:S(2)}, u32[]{:S(2)}) async-start(bf16[3,1024,768]{2,0,1:T(4,128)(2,1)} %copy.20), calls=%async_computation | async-start | bytes 12582912 | tf_op jit(solution)/shard_map/all_to_all | solution.py:125
  298.1 394.3 %reduce-scatter.2.cloned.1.call-start = ((), (), s32[]{:S(2)}) async-start(), calls=%async_computation.3 | async-start | bytes 15728640 | tf_op jit(solution)/shard_map/reduce_scatter | solution.py:134
  493.4 16.0 %copy-start.2 = (f32[128,48,128]{2,1,0:T(8,128)S(1)}, f32[128,48,128]{2,1,0:T(8,128)}, u32[]{:S(2)}) copy-start(f32[128,48,128]{2,1,0:T(8,128)} %copy.27) | copy-start | bytes 9437188
  526.4 4.8 copy-start.3
Sparse Core Ops, SparseCore 0:
  592.9 99.3 reduce-scatter.1

commit v2 on v1

v2 whole, which is shorter than its diff:
```python
import jax
import jax.numpy as jnp
from jax import lax
from jax.sharding import PartitionSpec as P


from jax.experimental import pallas as pl
from jax.experimental.pallas import tpu as pltpu

HALO = 136
CHUNK = 64
LANES = 128


def filter_kernel(halo_q, halo_k, halo_v, own_q, own_k, own_v, taps, medium, skip, out,
                  raw, prod, shifted, smooth_q):
    local = own_q.shape[0]
    ext = HALO + local
    taps_count = 7
    short_count = taps.shape[0] // 3

    def load_field(halo_ref, own_ref, slot):
        raw[slot, 0:HALO, :] = halo_ref[...].astype(jnp.float32)
        raw[slot, HALO:ext, :] = own_ref[...].astype(jnp.float32)

    load_field(halo_q, own_q, 0)
    load_field(halo_k, own_k, 1)
    load_field(halo_v, own_v, 2)

    def smooth(slot, first):
        total = jnp.zeros((ext - first, LANES), jnp.float32)
        for lag in range(taps_count):
            weight = taps[pl.ds(slot * short_count + lag, 1), :]
            total = total + weight * raw[slot, pl.ds(first - lag, ext - first), :]
        return total

    smooth_q[...] = smooth(0, HALO)
    prod[8:ext, :] = smooth(1, 8) * smooth(2, 8)
    for shift in range(8):
        shifted[shift, 16:ext, :] = prod[pl.ds(16 - shift, ext - 16), :]

    def chunk_body(index, carry):
        row = pl.multiple_of(index * CHUNK, CHUNK)
        at = pl.multiple_of(row + HALO, 8)
        total = skip[...] * prod[pl.ds(at, CHUNK), :]
        for group in range(medium.shape[0] // 8):
            base = pl.multiple_of(at - 8 * group, 8)
            for shift in range(8):
                weight = medium[pl.ds(8 * group + shift, 1), :]
                total = total + weight * shifted[shift, pl.ds(base, CHUNK), :]
        out[pl.ds(row, CHUNK), :] = (smooth_q[pl.ds(row, CHUNK), :] * total).astype(out.dtype)
        return carry

    lax.fori_loop(0, local // CHUNK, chunk_body, 0)


def channel_filter(halo, own, taps, medium, skip):
    local = own.shape[0]
    channels = own.shape[1] // 3
    tiles = channels // LANES
    ext = HALO + local

    def field_spec(rows, field):
        return pl.BlockSpec((rows, LANES), lambda t: (0, field * tiles + t))

    return pl.pallas_call(
        filter_kernel,
        grid=(tiles,),
        in_specs=[
            field_spec(HALO, 0),
            field_spec(HALO, 1),
            field_spec(HALO, 2),
            field_spec(local, 0),
            field_spec(local, 1),
            field_spec(local, 2),
            pl.BlockSpec((taps.shape[0], LANES), lambda t: (0, t)),
            pl.BlockSpec((medium.shape[0], LANES), lambda t: (0, t)),
            pl.BlockSpec((1, LANES), lambda t: (0, t)),
        ],
        out_specs=pl.BlockSpec((local, LANES), lambda t: (0, t)),
        out_shape=jax.ShapeDtypeStruct((local, channels), jnp.bfloat16),
        scratch_shapes=[
            pltpu.VMEM((3, ext, LANES), jnp.float32),
            pltpu.VMEM((ext, LANES), jnp.float32),
            pltpu.VMEM((8, ext, LANES), jnp.float32),
            pltpu.VMEM((local, LANES), jnp.float32),
        ],
    )(halo, halo, halo, own, own, own, taps, medium, skip)


def ring_order(count):
    if count % 2:
        return list(range(count))
    return list(range(0, count, 2)) + list(range(count - 1, 0, -2))


def ring_projection(tokens, in_weight):
    count = lax.axis_size("ctx")
    rows = in_weight.shape[0]
    order = ring_order(count)
    place = [0] * count
    for at, member in enumerate(order):
        place[member] = at
    forward = [(order[k], order[(k + 1) % count]) for k in range(count)]
    backward = [(order[k], order[(k - 1) % count]) for k in range(count)]
    me = lax.axis_index("ctx")
    order_table = jnp.array(order, jnp.int32)
    my_place = jnp.array(place, jnp.int32)[me]

    def partial(block, source, start, width):
        cols = lax.dynamic_slice_in_dim(tokens, source * rows + start, width, 1)
        return jnp.einsum("rd,dkc->rkc", cols, block, preferred_element_type=jnp.float32)

    total = partial(in_weight, me, 0, rows)
    full_steps = (count - 1) // 2
    half = rows // 2

    def sources(step):
        return (
            order_table[(my_place - step) % count],
            order_table[(my_place + step) % count],
        )

    def add_pair(total, ahead, behind, step):
        from_behind, from_ahead = sources(step)
        total = total + partial(ahead, from_behind, 0, rows)
        return total + partial(behind, from_ahead, 0, rows)

    def ring_step(step, carry):
        ahead, behind, total = carry
        moved_ahead = lax.ppermute(ahead, "ctx", forward)
        moved_behind = lax.ppermute(behind, "ctx", backward)
        total = add_pair(total, ahead, behind, step - 1)
        return (moved_ahead, moved_behind, total)

    if full_steps == 0:
        return total
    ahead = lax.ppermute(in_weight, "ctx", forward)
    behind = lax.ppermute(in_weight, "ctx", backward)
    ahead, behind, total = lax.fori_loop(
        2, full_steps + 1, ring_step, (ahead, behind, total)
    )
    if count % 2 == 0:
        last_ahead = lax.ppermute(ahead[:half], "ctx", forward)
        last_behind = lax.ppermute(behind[half:], "ctx", backward)
        total = add_pair(total, ahead, behind, full_steps)
        from_behind, from_ahead = sources(full_steps + 1)
        total = total + partial(last_ahead, from_behind, 0, half)
        total = total + partial(last_behind, from_ahead, half, rows - half)
    else:
        total = add_pair(total, ahead, behind, full_steps)
    return total


def per_device(tokens, in_weight, short_taps, medium_taps, medium_decay, skip_gain, out_weight):
    row_count = tokens.shape[0]
    channel_count = in_weight.shape[2]
    ctx_count = lax.axis_size("ctx")
    medium_count = medium_taps.shape[1]
    short_count = short_taps.shape[2]
    features = ring_projection(tokens, in_weight).astype(jnp.bfloat16)
    features = features.reshape(row_count, 3 * channel_count)
    halo = lax.ppermute(
        features[row_count - HALO :],
        "ctx",
        [(k, k + 1) for k in range(ctx_count - 1)],
    )
    lag_values = lax.broadcasted_iota(jnp.float32, (1, medium_count), 1)
    filters = medium_taps * jnp.exp(-medium_decay[:, None] * lag_values)
    taps = jnp.pad(
        jnp.transpose(short_taps, (0, 2, 1)), ((0, 0), (0, 8 - short_count), (0, 0))
    ).reshape(3 * 8, channel_count)
    gated = channel_filter(
        halo, features, taps, jnp.transpose(filters), skip_gain.reshape(1, channel_count)
    )
    summed = lax.psum_scatter(
        jnp.dot(gated, out_weight, preferred_element_type=jnp.float32),
        "tp",
        scatter_dimension=1,
        tiled=True,
    )
    return summed.astype(jnp.bfloat16)

def solution(mesh):
    return jax.shard_map(
        per_device,
        mesh=mesh,
        in_specs=(
            P("ctx", None),
            P("ctx", None, "tp"),
            P(None, "tp", None),
            P("tp", None),
            P("tp"),
            P("tp"),
            P("tp", None),
        ),
        out_specs=P("ctx", "tp"),
        check_vma=False,
    )
```

time: 711 us -> 474 us (0.67)
  local copies, waits for them, and re-layouts: 174 us -> 34.3 us
  other arithmetic: 49.6 us -> 4.18 us
  blocking collectives: 45 us -> 0 us
  Pallas kernels: 0 us -> 44.4 us
  matrix products: 115 us -> 81.6 us
  waiting for transfers between devices: 284 us -> 274 us
    reshape x3 -> x2, local copies, waits for them, and re-layouts: 62.6 us -> 7.27 us  [the longest x1 6.63 us: per_device(): features = features.reshape(row_count, 3 * channel_count)]
    all_to_all x1 -> x0, blocking collectives: 45 us -> none  [per_device(): lax.all_to_all(filtered, 'ctx', split_axis=1, concat_axis=0, tiled=True)]
    pallas_call x0 -> x1, Pallas kernels: none -> 44.4 us  [channel_filter(): pl.pallas_call(filter_kernel, grid=(tiles,), in_specs=[field_spec(HALO, 0...]
    unnamed x14 -> x12, local copies, waits for them, and re-layouts: 41.4 us -> 2.34 us
    dot_general x3 -> x1, matrix products: 45.6 us -> 12.2 us  [per_device(): jnp.dot(gated, out_weight, preferred_element_type=jnp.float32)]
    add x1 -> x0, other arithmetic: 30.6 us -> none  [channel_filter(): smoothed + short_weights[:, :, lag_step:lag_step + 1] * widened[:, :, sta...]
    slice x3 -> x1, local copies, waits for them, and re-layouts: 16.3 us -> 0.06 us  [per_device(): features[row_count - HALO:]]
    all_to_all x1 -> x0, waiting for transfers between devices: 12.1 us -> none  [per_device(): lax.all_to_all(tilted, 'ctx', split_axis=1, concat_axis=2, tiled=True)]
  transfers between devices with their start and end apart: 10 -> 10, of which waited for: 10 -> 9; matrix products, arithmetic and copies ran while one was open for 26% -> 16% of each run, Pallas kernels for 0% -> 0%
where the time goes in v2:
time: 474 us; the launch traced here: 473 us
  waiting for transfers between devices  274 us (58%)
  matrix products  81.6 us (17%)
  Pallas kernels  44.4 us (9%)
  local copies, waits for them, and re-layouts  34.3 us (7%)
  between operations  18.9 us (4%)
  starting transfers between devices  9.24 us (2%)
  loops' own time  5.6 us (1%)
    reduce_scatter x1, waiting for transfers between devices, per_device(): lax.psum_scatter(jnp.dot(gated, out_weight, preferred_element_type=jnp.fl...  103 us
    ppermute x2, waiting for transfers between devices, ring_step(): moved_ahead = lax.ppermute(ahead, 'ctx', forward)  99.4 us
    dot_general x9, matrix products, partial(): jnp.einsum('rd,dkc->rkc', cols, block, preferred_element_type=jnp.float32)  69.4 us
    ppermute x1, waiting for transfers between devices, ring_projection(): ahead = lax.ppermute(in_weight, 'ctx', forward)  58.3 us
    pallas_call x1, Pallas kernels, channel_filter(): pl.pallas_call(filter_kernel, grid=(tiles,), in_specs=[field_spec(HALO, 0...  44.4 us
    dot_general x1, matrix products, per_device(): jnp.dot(gated, out_weight, preferred_element_type=jnp.float32)  12.2 us
    while x12, local copies, waits for them, and re-layouts  11.5 us
  transfers between devices with their start and end apart: 10, of which 9 were waited for; matrix products, arithmetic and copies ran while one was open for 16% of the time, Pallas kernels for 0%

profile of v2, /device:TPU:1, one launch (start us, length us, event | category | flops | bytes accessed | tf_op | source)
XLA Modules:
  0.0 472.5 jit_solution(15794321300964549065)
XLA Ops:
  6.5 2.1 collective-permute-start.2
  8.7 1.3 dynamic_slice.83
  10.0 8.5 %fusion.11 = f32[768,3,1024]{2,0,1:T(8,128)} fusion(bf16[512,3,1024]{2,0,1:T(8,128)(2,1)} %param.12, bf16[768,4096]{1,0:T(8,128)(2,1)} %param.11, s32[]{:T(128)S(6)} %select_n.135), kind=kOutput, calls=%fused_computation.14 | convolution fusion | flops 2415919104 | bytes 13369348 | tf_op jit(solution)/shard_map/rd,dkc->rkc/dot_general | solution.py:112
  18.5 58.3 %collective-permute-done.2 = bf16[512,3,1024]{2,0,1:T(8,128)(2,1)} collective-permute-done((bf16[512,3,1024]{2,0,1:T(8,128)(2,1)}, bf16[512,3,1024]{2,0,1:T(8,128)(2,1)}, u32[]{:S(2)}, u32[]{:S(2)}) %collective-permute-start.2) | collective-permute-done | bytes 3145760 | tf_op jit(solution)/shard_map/ppermute | solution.py:138
  76.7 0.9 collective-permute-done.3
  77.6 148.0 %while.22 = (s32[]{:T(128)}, bf16[512,3,1024]{2,0,1:T(8,128)(2,1)}, bf16[512,3,1024]{2,0,1:T(8,128)(2,1)}, f32[768,3,1024]{2,0,1:T(8,128)}, s32[]{:T(128)}, /*in...) while((s32[]{:T(128)}, bf16[512,3,1024]{2,0,1:T(8,128)(2,1)}, ...), condition=%wide.region_1.2_spmd.clone, body=%wide.region_0.1_spmd.sunk.clone.sunk | while | flops 4836556800 | bytes 158859952 | solution.py:140
  77.6 3.8 copy.25
  81.5 1.3 collective-permute-start
  82.8 1.9 copy.26
  84.7 0.2 collective-permute-start.1
  86.3 0.7 fusion.51
  88.3 4.9 %fusion.52 = f32[768,3,1024]{2,0,1:T(8,128)S(1)} fusion(bf16[512,3,1024]{2,0,1:T(8,128)(2,1)} %copy.25, bf16[768,4096]{1,0:T(8,128)(2,1)} %get-tuple-element.351, s32[]{:T(128)S(6)} %select_n.171), kind=kOutput, calls=%fused_computation.2.clone.1 | convolution fusion | flops 2415919104 | bytes 13369348 | tf_op jit(solution)/shard_map/while/body/eval_jaxpr/rd,dkc->rkc/dot_general | solution.py:112
  93.2 6.0 %add_add_fusion.2 = f32[768,3,1024]{2,0,1:T(8,128)S(1)} fusion(f32[768,3,1024]{2,0,1:T(8,128)S(1)} %copy-done, f32[768,3,1024]{2,0,1:T(8,128)S(1)} %fusion.52, bf16[512,3,1024]{2,0,1:T(8,128)(2,1)S(1)} %copy.26, bf16[768,4096]{1,0:T(8,128)(2,1)} %get-tuple-element.351, s32[]{:T(128)S(6)} %select_n.172), kind=kOutput, calls=%fused_computation.clone.1 | convolution fusion | flops 2420637696 | bytes 32243716 | tf_op jit(solution)/shard_map/while/body/eval_jaxpr/rd,dkc->rkc/dot_general | solution.py:112
  99.3 50.3 %collective-permute-done = bf16[512,3,1024]{2,0,1:T(8,128)(2,1)} collective-permute-done((bf16[512,3,1024]{2,0,1:T(8,128)(2,1)}, bf16[512,3,1024]{2,0,1:T(8,128)(2,1)}, u32[]{:S(2)}, u32[]{:S(2)}) %collective-permute-start) | collective-permute-done | bytes 3145760 | tf_op jit(solution)/shard_map/while/body/eval_jaxpr/ppermute | solution.py:131
  149.5 2.7 collective-permute-done.1
  152.2 3.8 copy.25
  156.1 1.3 collective-permute-start
  157.4 1.9 copy.26
  159.3 0.2 collective-permute-start.1
  160.8 0.7 fusion.51
  162.9 4.9 %fusion.52 = f32[768,3,1024]{2,0,1:T(8,128)S(1)} fusion(bf16[512,3,1024]{2,0,1:T(8,128)(2,1)} %copy.25, bf16[768,4096]{1,0:T(8,128)(2,1)} %get-tuple-element.351, s32[]{:T(128)S(6)} %select_n.171), kind=kOutput, calls=%fused_computation.2.clone.1 | convolution fusion | flops 2415919104 | bytes 13369348 | tf_op jit(solution)/shard_map/while/body/eval_jaxpr/rd,dkc->rkc/dot_general | solution.py:112
  167.8 6.0 %add_add_fusion.2 = f32[768,3,1024]{2,0,1:T(8,128)S(1)} fusion(f32[768,3,1024]{2,0,1:T(8,128)S(1)} %copy-done, f32[768,3,1024]{2,0,1:T(8,128)S(1)} %fusion.52, bf16[512,3,1024]{2,0,1:T(8,128)(2,1)S(1)} %copy.26, bf16[768,4096]{1,0:T(8,128)(2,1)} %get-tuple-element.351, s32[]{:T(128)S(6)} %select_n.172), kind=kOutput, calls=%fused_computation.clone.1 | convolution fusion | flops 2420637696 | bytes 32243716 | tf_op jit(solution)/shard_map/while/body/eval_jaxpr/rd,dkc->rkc/dot_general | solution.py:112
  173.8 49.1 %collective-permute-done = bf16[512,3,1024]{2,0,1:T(8,128)(2,1)} collective-permute-done((bf16[512,3,1024]{2,0,1:T(8,128)(2,1)}, bf16[512,3,1024]{2,0,1:T(8,128)(2,1)}, u32[]{:S(2)}, u32[]{:S(2)}) %collective-permute-start) | collective-permute-done | bytes 3145760 | tf_op jit(solution)/shard_map/while/body/eval_jaxpr/ppermute | solution.py:131
  222.9 2.7 collective-permute-done.1
  225.6 1.5 slice.12
  227.1 1.3 collective-permute-start.4
  231.3 0.7 fusion.30
  234.5 1.5 slice.13
  236.0 0.5 collective-permute-start.5
  236.5 8.4 %fusion.7 = f32[768,3,1024]{2,0,1:T(8,128)} fusion(bf16[512,3,1024]{2,0,1:T(8,128)(2,1)} %get-tuple-element.239, bf16[768,4096]{1,0:T(8,128)(2,1)} %get-tuple-element.364, s32[]{:T(128)S(6)} %select_n.142), kind=kOutput, calls=%fused_computation.10 | convolution fusion | flops 2415919104 | bytes 13369348 | tf_op jit(solution)/shard_map/rd,dkc->rkc/dot_general | solution.py:112
  244.9 8.4 %fusion.9 = f32[768,3,1024]{2,0,1:T(8,128)} fusion(bf16[512,3,1024]{2,0,1:T(8,128)(2,1)} %get-tuple-element.238, bf16[768,4096]{1,0:T(8,128)(2,1)} %get-tuple-element.364, s32[]{:T(128)S(6)} %select_n.139), kind=kOutput, calls=%fused_computation.12 | convolution fusion | flops 2415919104 | bytes 13369348 | tf_op jit(solution)/shard_map/rd,dkc->rkc/dot_general | solution.py:112
  253.3 5.6 %collective-permute-done.4 = bf16[256,3,1024]{2,0,1:T(8,128)(2,1)} collective-permute-done((bf16[256,3,1024]{2,0,1:T(8,128)(2,1)S(1)}, bf16[256,3,1024]{2,0,1:T(8,128)(2,1)}, u32[]{:S(2)}, u32[]{:S(2)}) %collective-permute-start.4) | collective-permute-done | bytes 1572896 | tf_op jit(solution)/shard_map/ppermute | solution.py:144
  258.9 6.6 %fusion.20 = f32[768,3,1024]{2,0,1:T(8,128)} fusion(bf16[256,3,1024]{2,0,1:T(8,128)(2,1)} %collective-permute-done.4, bf16[768,4096]{1,0:T(8,128)(2,1)} %get-tuple-element.364, s32[]{:T(128)S(6)} %select_n.145), kind=kOutput, calls=%fused_computation.22 | convolution fusion | flops 1207959552 | bytes 11403268 | tf_op jit(solution)/shard_map/rd,dkc->rkc/dot_general | solution.py:112
  265.5 2.1 collective-permute-done.5
  267.6 15.6 %add_convert_fusion = bf16[768,3,1024]{2,0,1:T(8,128)(2,1)} fusion(f32[768,3,1024]{2,0,1:T(8,128)} %fusion.20, f32[768,3,1024]{2,0,1:T(8,128)} %fusion.7, f32[768,3,1024]{2,0,1:T(8,128)} %get-tuple-element.237, f32[768,3,1024]{2,0,1:T(8,128)} %fusion.9, bf16[256,3,1024]{2,0,1:T(8,128)(2,1)S(1)} %collective-permute-done.5, ...), kind=kOutput, calls=%fused_computation.8 | convolution fusion | flops 1219756032 | bytes 44433412 | tf_op jit(solution)/shard_map/rd,dkc->rkc/dot_general | solution.py:112
  283.3 1.2 slice_bitcast_fusion
  284.5 0.1 copy.19
  284.5 2.4 collective-permute-start.6
  287.0 0.2 copy.15
  287.2 0.6 pad_bitcast_fusion.taps
  287.9 0.9 multiply_bitcast_fusion.medium
  288.8 6.7 %copy.14 = bf16[768,3,1024]{0,2,1:T(8,128)(2,1)} copy(bf16[768,3,1024]{2,0,1:T(8,128)(2,1)} %add_convert_fusion) | data formatting | bytes 9437184 | tf_op jit(solution)/shard_map/convert_element_type | solution.py:161
  295.5 6.6 %copy.16.own_q.own_k.own_v = bf16[768,3072]{1,0:T(8,128)(2,1)} copy(bf16[768,3072]{0,1:T(8,128)(2,1)} %bitcast.62) | data formatting | bytes 9437184 | tf_op jit(solution)/shard_map/reshape | solution.py:162
  302.1 0.9 copy-done.2
  303.0 44.4 %shard_map.91 = bf16[768,1024]{1,0:T(8,128)(2,1)} custom-call(bf16[136,3072]{1,0:T(8,128)(2,1)} %copy-done.2, bf16[136,3072]{1,0:T(8,128)(2,1)} %copy-done.2, bf16[136,3072]{1,0:T(8,128)(2,1)} %copy-done.2, bf16[768,3072]{1,0:T(8,128)(2,1)} %copy.16.own_q.own_k.own_v, bf16[768,3072]{1,0:T(8,128)(2,1)} %copy.16.own_q.own_k.own_v, ...), custom_call_target="tpu_custom_call" | custom-call | tf_op jit(solution)/shard_map/pallas_call | solution.py:66
  347.4 12.2 %fusion.31 = f32[768,4096]{1,0:T(8,128)} fusion(bf16[768,1024]{1,0:T(8,128)(2,1)} %shard_map.91, bf16[1024,4096]{1,0:T(8,128)(2,1)} %param.17), kind=kOutput, calls=%fused_computation.34 | convolution fusion | flops 6442450944 | bytes 22544384 | tf_op jit(solution)/shard_map/dot_general | solution.py:177
  359.7 102.8 %reduce-scatter.2.cloned.1.call-done = f32[768,1024]{1,0:T(8,128)} async-done(((f32[768,4096]{1,0:T(8,128)}), f32[768,1024]{1,0:T(8,128)}) %reduce-scatter.2.cloned.1.call-update) | async-done | bytes 3145744 | tf_op jit(solution)/shard_map/reduce_scatter | solution.py:176
  462.4 3.3 convert_element_type.9
  (22 shorter events, 0.1 us)
Async XLA Ops:
  6.5 455.9 %reduce-scatter.2.cloned.1.call-start = ((), (), s32[]{:S(2)}) async-start(), calls=%async_computation.1 | async-start | bytes 15728640 | tf_op jit(solution)/shard_map/reduce_scatter | solution.py:176
  6.5 70.2 %collective-permute-start.2 = (bf16[512,3,1024]{2,0,1:T(8,128)(2,1)}, bf16[512,3,1024]{2,0,1:T(8,128)(2,1)}, u32[]{:S(2)}, u32[]{:S(2)}) collective-permute-start(bf16[512,3,1024]{2,0,1:T(8,128)(2,1)} %param.12), channel_id=1, source_target_pairs={{0,8},{8,16},{16,24},{24,28},{28,20},{20,12},{12,4},{4,0},{1,9},{9... | collective-permute-start | bytes 9437192 | tf_op jit(solution)/shard_map/ppermute | solution.py:138
  8.7 69.0 %collective-permute-start.3 = (bf16[512,3,1024]{2,0,1:T(8,128)(2,1)}, bf16[512,3,1024]{2,0,1:T(8,128)(2,1)}, u32[]{:S(2)}, u32[]{:S(2)}) collective-permute-start(bf16[512,3,1024]{2,0,1:T(8,128)(2,1)} %param.12), channel_id=1, source_target_pairs={{0,4},{8,0},{16,8},{24,16},{28,24},{20,28},{12,20},{4,12},{1,5},{9... | collective-permute-start | bytes 9437192 | tf_op jit(solution)/shard_map/ppermute | solution.py:139
  10.0 67.6 %copy-start.4 = (s32[8]{0:T(128)S(1)}, s32[8]{0:T(128)}, u32[]{:S(2)}) copy-start(s32[8]{0:T(128)} %constant.157.clone) | copy-start | bytes 100
  81.5 68.0 %collective-permute-start = (bf16[512,3,1024]{2,0,1:T(8,128)(2,1)}, bf16[512,3,1024]{2,0,1:T(8,128)(2,1)}, u32[]{:S(2)}, u32[]{:S(2)}) collective-permute-start(bf16[512,3,1024]{2,0,1:T(8,128)(2,1)} %copy.25), channel_id=1, source_target_pairs={{0,8},{8,16},{16,24},{24,28},{28,20},{20,12},{12,4},{4,0},{1,9},{9... | collective-permute-start | bytes 9437192 | tf_op jit(solution)/shard_map/while/body/eval_jaxpr/ppermute | solution.py:131
  84.7 67.6 %collective-permute-start.1 = (bf16[512,3,1024]{2,0,1:T(8,128)(2,1)S(1)}, bf16[512,3,1024]{2,0,1:T(8,128)(2,1)}, u32[]{:S(2)}, u32[]{:S(2)}) collective-permute-start(bf16[512,3,1024]{2,0,1:T(8,128)(2,1)S(1)} %copy.26), channel_id=1, source_target_pairs={{0,4},{8,0},{16,8},{24,16},{28,24},{20,28},{12,20},{4,12},{1,5},{9... | collective-permute-start | bytes 9437192 | tf_op jit(solution)/shard_map/while/body/eval_jaxpr/ppermute | solution.py:132
  88.3 4.9 %copy-start = (f32[768,3,1024]{2,0,1:T(8,128)S(1)}, f32[768,3,1024]{2,0,1:T(8,128)}, u32[]{:S(2)}) copy-start(f32[768,3,1024]{2,0,1:T(8,128)} %get-tuple-element.336) | copy-start | bytes 28311556 | tf_op jit(solution)/shard_map/while
  99.2 53.0 %copy-start.1 = (f32[768,3,1024]{2,0,1:T(8,128)}, f32[768,3,1024]{2,0,1:T(8,128)S(1)}, u32[]{:S(2)}) copy-start(f32[768,3,1024]{2,0,1:T(8,128)S(1)} %add_add_fusion.2) | copy-start | bytes 28311556 | tf_op jit(solution)/shard_map/while
  156.1 66.8 %collective-permute-start = (bf16[512,3,1024]{2,0,1:T(8,128)(2,1)}, bf16[512,3,1024]{2,0,1:T(8,128)(2,1)}, u32[]{:S(2)}, u32[]{:S(2)}) collective-permute-start(bf16[512,3,1024]{2,0,1:T(8,128)(2,1)} %copy.25), channel_id=1, source_target_pairs={{0,8},{8,16},{16,24},{24,28},{28,20},{20,12},{12,4},{4,0},{1,9},{9... | collective-permute-start | bytes 9437192 | tf_op jit(solution)/shard_map/while/body/eval_jaxpr/ppermute | solution.py:131
  159.3 66.4 %collective-permute-start.1 = (bf16[512,3,1024]{2,0,1:T(8,128)(2,1)S(1)}, bf16[512,3,1024]{2,0,1:T(8,128)(2,1)}, u32[]{:S(2)}, u32[]{:S(2)}) collective-permute-start(bf16[512,3,1024]{2,0,1:T(8,128)(2,1)S(1)} %copy.26), channel_id=1, source_target_pairs={{0,4},{8,0},{16,8},{24,16},{28,24},{20,28},{12,20},{4,12},{1,5},{9... | collective-permute-start | bytes 9437192 | tf_op jit(solution)/shard_map/while/body/eval_jaxpr/ppermute | solution.py:132
  162.9 4.9 %copy-start = (f32[768,3,1024]{2,0,1:T(8,128)S(1)}, f32[768,3,1024]{2,0,1:T(8,128)}, u32[]{:S(2)}) copy-start(f32[768,3,1024]{2,0,1:T(8,128)} %get-tuple-element.336) | copy-start | bytes 28311556 | tf_op jit(solution)/shard_map/while
  173.8 51.8 %copy-start.1 = (f32[768,3,1024]{2,0,1:T(8,128)}, f32[768,3,1024]{2,0,1:T(8,128)S(1)}, u32[]{:S(2)}) copy-start(f32[768,3,1024]{2,0,1:T(8,128)S(1)} %add_add_fusion.2) | copy-start | bytes 28311556 | tf_op jit(solution)/shard_map/while
  227.1 31.8 %collective-permute-start.4 = (bf16[256,3,1024]{2,0,1:T(8,128)(2,1)S(1)}, bf16[256,3,1024]{2,0,1:T(8,128)(2,1)}, u32[]{:S(2)}, u32[]{:S(2)}) collective-permute-start(bf16[256,3,1024]{2,0,1:T(8,128)(2,1)S(1)} %slice.12), channel_id=1, source_target_pairs={{0,8},{8,16},{16,24},{24,28},{28,20},{20,12},{12,4},{4,0},{1,9},{9... | collective-permute-start | bytes 4718600 | tf_op jit(solution)/shard_map/ppermute | solution.py:144
  236.0 31.6 %collective-permute-start.5 = (bf16[256,3,1024]{2,0,1:T(8,128)(2,1)S(1)}, bf16[256,3,1024]{2,0,1:T(8,128)(2,1)S(1)}, u32[]{:S(2)}, u32[]{:S(2)}) collective-permute-start(bf16[256,3,1024]{2,0,1:T(8,128)(2,1)S(1)} %slice.13), channel_id=1, source_target_pairs={{0,4},{8,0},{16,8},{24,16},{28,24},{20,28},{12,20},{4,12},{1,5},{9... | collective-permute-start | bytes 4718600 | tf_op jit(solution)/shard_map/ppermute | solution.py:145
  267.6 19.3 %copy-start.3 = (f32[1024,128]{1,0:T(8,128)S(1)}, f32[1024,128]{1,0:T(8,128)}, u32[]{:S(2)}) copy-start(f32[1024,128]{1,0:T(8,128)} %param.14) | copy-start | bytes 1572868
  267.6 19.5 %copy-start.6 = (f32[1024]{0:T(1024)S(1)}, f32[1024]{0:T(1024)}, u32[]{:S(2)}) copy-start(f32[1024]{0:T(1024)} %param.15) | copy-start | bytes 12292
  267.6 19.6 %copy-start.5 = (f32[3,1024,7]{1,2,0:T(8,128)S(1)}, f32[3,1024,7]{1,2,0:T(8,128)}, u32[]{:S(2)}) copy-start(f32[3,1024,7]{1,2,0:T(8,128)} %param.13) | copy-start | bytes 258052
  284.5 17.6 %collective-permute-start.6 = (bf16[136,3072]{1,0:T(8,128)(2,1)S(1)}, bf16[136,3072]{1,0:T(8,128)(2,1)S(1)}, u32[]{:S(2)}, u32[]{:S(2)}) collective-permute-start(bf16[136,3072]{1,0:T(8,128)(2,1)S(1)} %bitcast.63), channel_id=1, source_target_pairs={{0,4},{4,8},{8,12},{12,16},{16,20},{20,24},{24,28},{1,5},{5,9},{9,... | collective-permute-start | bytes 2506760 | tf_op jit(solution)/shard_map/ppermute | solution.py:163
  302.1 0.9 copy-start.2
Sparse Core Ops, SparseCore 0:
  359.8 102.5 reduce-scatter.1

commit v3 on v2

--- a/solution.py
+++ b/solution.py
@@ -94,7 +94,7 @@
     return list(range(0, count, 2)) + list(range(count - 1, 0, -2))
 
 
-def ring_projection(tokens, in_weight):
+def ring_projection(tokens, in_weight, riders):
     count = lax.axis_size("ctx")
     rows = in_weight.shape[0]
     order = ring_order(count)
@@ -134,12 +134,19 @@
         return (moved_ahead, moved_behind, total)
 
     if full_steps == 0:
-        return total
+        return total, riders
     ahead = lax.ppermute(in_weight, "ctx", forward)
     behind = lax.ppermute(in_weight, "ctx", backward)
-    ahead, behind, total = lax.fori_loop(
-        2, full_steps + 1, ring_step, (ahead, behind, total)
-    )
+    carry = (ahead, behind, total)
+    if full_steps >= 2:
+        carry = ring_step(2, carry)
+    carry, riders = lax.optimization_barrier((carry, riders))
+
+    def carried_step(step, state):
+        return (ring_step(step, state[0]), state[1])
+
+    carry, riders = lax.fori_loop(3, full_steps + 1, carried_step, (carry, riders))
+    ahead, behind, total = carry
     if count % 2 == 0:
         last_ahead = lax.ppermute(ahead[:half], "ctx", forward)
         last_behind = lax.ppermute(behind[half:], "ctx", backward)
@@ -149,8 +156,42 @@
         total = total + partial(last_behind, from_ahead, half, rows - half)
     else:
         total = add_pair(total, ahead, behind, full_steps)
+    return total, riders
+
+
+def tp_bits(count):
+    bits = []
+    bit = 1
+    while bit < count:
+        bits.append(bit)
+        bit *= 2
+    return bits
+
+
+def spread_weights(out_weight):
+    count = lax.axis_size("tp")
+    me = lax.axis_index("tp")
+    width = out_weight.shape[1] // count
+    weights = [lax.dynamic_slice_in_dim(out_weight, me * width, width, 1)]
+    for partner in range(1, count):
+        pairs = [(k, k ^ partner) for k in range(count)]
+        sent = lax.dynamic_slice_in_dim(out_weight, (me ^ partner) * width, width, 1)
+        weights.append(lax.ppermute(sent, "tp", pairs))
+    return tuple(weights)
+
+
+def output_projection(gated, weights):
+    count = lax.axis_size("tp")
+    pieces = {0: gated}
+    for bit in reversed(tp_bits(count)):
+        pairs = [(k, k ^ bit) for k in range(count)]
+        moved = {key ^ bit: lax.ppermute(piece, "tp", pairs) for key, piece in pieces.items()}
+        pieces.update(moved)
+    total = None
+    for key in sorted(pieces):
+        part = jnp.dot(pieces[key], weights[key], preferred_element_type=jnp.float32)
+        total = part if total is None else total + part
     return total
-
 
 def per_device(tokens, in_weight, short_taps, medium_taps, medium_decay, skip_gain, out_weight):
     row_count = tokens.shape[0]
@@ -158,7 +199,8 @@
     ctx_count = lax.axis_size("ctx")
     medium_count = medium_taps.shape[1]
     short_count = short_taps.shape[2]
-    features = ring_projection(tokens, in_weight).astype(jnp.bfloat16)
+    features, weights = ring_projection(tokens, in_weight, spread_weights(out_weight))
+    features = features.astype(jnp.bfloat16)
     features = features.reshape(row_count, 3 * channel_count)
     halo = lax.ppermute(
         features[row_count - HALO :],
@@ -173,13 +215,7 @@
     gated = channel_filter(
         halo, features, taps, jnp.transpose(filters), skip_gain.reshape(1, channel_count)
     )
-    summed = lax.psum_scatter(
-        jnp.dot(gated, out_weight, preferred_element_type=jnp.float32),
-        "tp",
-        scatter_dimension=1,
-        tiled=True,
-    )
-    return summed.astype(jnp.bfloat16)
+    return output_projection(gated, weights).astype(jnp.bfloat16)
 
 def solution(mesh):
     return jax.shard_map(

time: 474 us -> 436 us (0.920)
  waiting for transfers between devices: 274 us -> 237 us
  starting transfers between devices: 9.24 us -> 21.6 us
  between operations: 18.9 us -> 10.5 us
  matrix products: 81.6 us -> 89.2 us
  loops' own time: 5.6 us -> 0 us
  local copies, waits for them, and re-layouts: 34.3 us -> 28.7 us
    reduce_scatter x1 -> x0, waiting for transfers between devices: 103 us -> none  [per_device(): lax.psum_scatter(jnp.dot(gated, out_weight, preferred_element_type=jnp.fl...]
    ppermute x0 -> x6, waiting for transfers between devices: none -> 93.1 us  [the longest x3 65 us: spread_weights(): weights.append(lax.ppermute(sent, 'tp', pairs))]
    ppermute x2, waiting for transfers between devices: 99.4 us -> 64.3 us  [ring_step(): moved_ahead = lax.ppermute(ahead, 'ctx', forward)]
    ppermute x0 -> x6, starting transfers between devices: none -> 12.3 us  [the longest x3 8.9 us: output_projection(): lax.ppermute(piece, 'tp', pairs)]
    while x12 -> x0, local copies, waits for them, and re-layouts: 11.5 us -> none
    ppermute x1, waiting for transfers between devices: 58.3 us -> 68.1 us  [ring_projection(): ahead = lax.ppermute(in_weight, 'ctx', forward)]
    dynamic_slice x0 -> x1, local copies, waits for them, and re-layouts: none -> 7.07 us  [spread_weights(): lax.dynamic_slice_in_dim(out_weight, (me ^ partner) * width, width, 1)]
    another operation x1 -> x0, loops' own time: 5.6 us -> none  [ring_projection(): lax.fori_loop(2, full_steps + 1, ring_step, (ahead, behind, total))]
  transfers between devices with their start and end apart: 10 -> 15, of which waited for: 9 -> 8; matrix products, arithmetic and copies ran while one was open for 16% -> 20% of each run, Pallas kernels for 0% -> 0%
where the time goes in v3:
time: 436 us; the launch traced here: 433 us
  waiting for transfers between devices  237 us (54%)
  matrix products  89.2 us (20%)
  Pallas kernels  44.6 us (10%)
  local copies, waits for them, and re-layouts  28.7 us (7%)
  starting transfers between devices  21.6 us (5%)
  between operations  10.5 us (2%)
    dot_general x9, matrix products, partial(): jnp.einsum('rd,dkc->rkc', cols, block, preferred_element_type=jnp.float32)  74.6 us
    ppermute x1, waiting for transfers between devices, ring_projection(): ahead = lax.ppermute(in_weight, 'ctx', forward)  68.1 us
    ppermute x3, waiting for transfers between devices, spread_weights(): weights.append(lax.ppermute(sent, 'tp', pairs))  65 us
    ppermute x2, waiting for transfers between devices, ring_step(): moved_ahead = lax.ppermute(ahead, 'ctx', forward)  64.3 us
    pallas_call x1, Pallas kernels, channel_filter(): pl.pallas_call(filter_kernel, grid=(tiles,), in_specs=[field_spec(HALO, 0...  44.6 us
    ppermute x3, waiting for transfers between devices, output_projection(): lax.ppermute(piece, 'tp', pairs)  28.1 us
    dot_general x4, matrix products, output_projection(): jnp.dot(pieces[key], weights[key], preferred_element_type=jnp.float32)  14.6 us
    ppermute x3, starting transfers between devices, output_projection(): lax.ppermute(piece, 'tp', pairs)  8.9 us
  transfers between devices with their start and end apart: 15, of which 8 were waited for; matrix products, arithmetic and copies ran while one was open for 20% of the time, Pallas kernels for 0%

profile of v3, /device:TPU:1, one launch (start us, length us, event | category | flops | bytes accessed | tf_op | source)
XLA Modules:
  0.0 432.9 jit_solution(15694880138031889241)
XLA Ops:
  0.0 2.1 collective-permute-start
  2.1 68.1 %collective-permute-done = bf16[512,3,1024]{2,0,1:T(8,128)(2,1)} collective-permute-done((bf16[512,3,1024]{2,0,1:T(8,128)(2,1)}, bf16[512,3,1024]{2,0,1:T(8,128)(2,1)}, u32[]{:S(2)}, u32[]{:S(2)}) %collective-permute-start) | collective-permute-done | bytes 3145760 | tf_op jit(solution)/shard_map/ppermute | solution.py:138
  70.2 1.2 collective-permute-start.1
  71.4 0.3 collective-permute-start.3
  71.7 7.1 %constant_dynamic-slice_fusion = (bf16[1024,1024]{1,0:T(8,128)(2,1)}, bf16[1024,1024]{1,0:T(8,128)(2,1)}, bf16[1024,1024]{1,0:T(8,128)(2,1)}, bf16[1024,1024]{1,0:T(8,128)(2,1)}) fusion(bf16[1024,4096]{1,0:T(8,128)(2,1)} %param.15, s32[]{:T(128)S(6)} %select_n.119, s32[]{:T(128)S(6)} %select_n.117, s32[]{:T(128)S(6)} %select_n.116, s32[]{:T(128)S(6)} %select_n.118), kind=kLoop, calls=%fused_computation.38 | loop fusion | bytes 16777232 | tf_op jit(solution)/shard_map/dynamic_slice | solution.py:178
  78.8 1.8 collective-permute-start.4
  80.5 1.4 collective-permute-start.5
  82.0 0.2 collective-permute-start.6
  82.2 0.6 dynamic_slice.71
  88.1 0.7 fusion.37
  89.9 4.8 %fusion.13 = f32[768,3,1024]{2,0,1:T(8,128)S(1)} fusion(bf16[512,3,1024]{2,0,1:T(8,128)(2,1)} %param.10, bf16[768,4096]{1,0:T(8,128)(2,1)} %param.9, s32[]{:T(128)S(6)} %select_n.108), kind=kOutput, calls=%fused_computation.15 | convolution fusion | flops 2415919104 | bytes 13369348 | tf_op jit(solution)/shard_map/rd,dkc->rkc/dot_general | solution.py:112
  94.7 4.8 %fusion.11 = f32[768,3,1024]{2,0,1:T(8,128)S(1)} fusion(bf16[512,3,1024]{2,0,1:T(8,128)(2,1)} %collective-permute-done, bf16[768,4096]{1,0:T(8,128)(2,1)} %param.9, s32[]{:T(128)S(6)} %select_n.112), kind=kOutput, calls=%fused_computation.13 | convolution fusion | flops 2415919104 | bytes 13369348 | tf_op jit(solution)/shard_map/rd,dkc->rkc/dot_general | solution.py:112
  99.4 8.7 %add_add_fusion = f32[768,3,1024]{2,0,1:T(8,128)} fusion(f32[768,3,1024]{2,0,1:T(8,128)S(1)} %fusion.13, f32[768,3,1024]{2,0,1:T(8,128)S(1)} %fusion.11, bf16[512,3,1024]{2,0,1:T(8,128)(2,1)} %collective-permute-done.2, bf16[768,4096]{1,0:T(8,128)(2,1)} %param.9, s32[]{:T(128)S(6)} %select_n.115), kind=kOutput, calls=%fused_computation.1 | convolution fusion | flops 2420637696 | bytes 32243716 | tf_op jit(solution)/shard_map/rd,dkc->rkc/dot_general | solution.py:112
  108.2 20.0 %collective-permute-done.5 = bf16[1024,1024]{1,0:T(8,128)(2,1)} collective-permute-done((bf16[1024,1024]{1,0:T(8,128)(2,1)}, bf16[1024,1024]{1,0:T(8,128)(2,1)}, u32[]{:S(2)}, u32[]{:S(2)}) %collective-permute-start.5) | collective-permute-done | bytes 2097184 | tf_op jit(solution)/shard_map/ppermute | solution.py:179
  128.1 45.0 %collective-permute-done.6 = bf16[1024,1024]{1,0:T(8,128)(2,1)} collective-permute-done((bf16[1024,1024]{1,0:T(8,128)(2,1)}, bf16[1024,1024]{1,0:T(8,128)(2,1)}, u32[]{:S(2)}, u32[]{:S(2)}) %collective-permute-start.6) | collective-permute-done | bytes 2097184 | tf_op jit(solution)/shard_map/ppermute | solution.py:179
  173.2 1.5 collective-permute-start.7
  178.5 64.3 %collective-permute-done.7 = bf16[512,3,1024]{2,0,1:T(8,128)(2,1)} collective-permute-done((bf16[512,3,1024]{2,0,1:T(8,128)(2,1)}, bf16[512,3,1024]{2,0,1:T(8,128)(2,1)}, u32[]{:S(2)}, u32[]{:S(2)}) %collective-permute-start.7) | collective-permute-done | bytes 3145760 | tf_op jit(solution)/shard_map/while/body/eval_jaxpr/ppermute | solution.py:131
  242.9 1.5 slice.16
  244.4 1.6 collective-permute-start.9
  246.0 8.4 %fusion.8 = f32[768,3,1024]{2,0,1:T(8,128)} fusion(bf16[512,3,1024]{2,0,1:T(8,128)(2,1)} %collective-permute-done.1, bf16[768,4096]{1,0:T(8,128)(2,1)} %param.9, s32[]{:T(128)S(6)} %select_n.122), kind=kOutput, calls=%fused_computation.10 | convolution fusion | flops 2415919104 | bytes 13369348 | tf_op jit(solution)/shard_map/while/body/eval_jaxpr/rd,dkc->rkc/dot_general | solution.py:112
  254.4 1.5 slice.17
  255.9 0.2 collective-permute-start.10
  256.2 8.5 %fusion = f32[768,3,1024]{2,0,1:T(8,128)} fusion(bf16[512,3,1024]{2,0,1:T(8,128)(2,1)} %collective-permute-done.8, bf16[768,4096]{1,0:T(8,128)(2,1)} %param.9, s32[]{:T(128)S(6)} %select_n.131), kind=kOutput, calls=%fused_computation.4 | convolution fusion | flops 2415919104 | bytes 13369348 | tf_op jit(solution)/shard_map/rd,dkc->rkc/dot_general | solution.py:112
  264.6 8.4 %fusion.2 = f32[768,3,1024]{2,0,1:T(8,128)} fusion(bf16[512,3,1024]{2,0,1:T(8,128)(2,1)} %collective-permute-done.7, bf16[768,4096]{1,0:T(8,128)(2,1)} %param.9, s32[]{:T(128)S(6)} %select_n.128), kind=kOutput, calls=%fused_computation.6 | convolution fusion | flops 2415919104 | bytes 13369348 | tf_op jit(solution)/shard_map/rd,dkc->rkc/dot_general | solution.py:112
  273.0 6.2 %collective-permute-done.9 = bf16[256,3,1024]{2,0,1:T(8,128)(2,1)S(1)} collective-permute-done((bf16[256,3,1024]{2,0,1:T(8,128)(2,1)S(1)}, bf16[256,3,1024]{2,0,1:T(8,128)(2,1)S(1)}, u32[]{:S(2)}, u32[]{:S(2)}) %collective-permute-start.9) | collective-permute-done | bytes 1572896 | tf_op jit(solution)/shard_map/ppermute | solution.py:151
  279.2 6.0 %fusion.24 = f32[768,3,1024]{2,0,1:T(8,128)} fusion(bf16[256,3,1024]{2,0,1:T(8,128)(2,1)S(1)} %collective-permute-done.9, bf16[768,4096]{1,0:T(8,128)(2,1)} %param.9, s32[]{:T(128)S(6)} %select_n.134), kind=kOutput, calls=%fused_computation.27 | convolution fusion | flops 1207959552 | bytes 11403268 | tf_op jit(solution)/shard_map/rd,dkc->rkc/dot_general | solution.py:112
  285.2 5.4 %collective-permute-done.10 = bf16[256,3,1024]{2,0,1:T(8,128)(2,1)S(1)} collective-permute-done((bf16[256,3,1024]{2,0,1:T(8,128)(2,1)S(1)}, bf16[256,3,1024]{2,0,1:T(8,128)(2,1)S(1)}, u32[]{:S(2)}, u32[]{:S(2)}) %collective-permute-start.10) | collective-permute-done | bytes 1572896 | tf_op jit(solution)/shard_map/ppermute | solution.py:152
  290.6 6.0 %fusion.22 = f32[768,3,1024]{2,0,1:T(8,128)} fusion(bf16[256,3,1024]{2,0,1:T(8,128)(2,1)S(1)} %collective-permute-done.10, bf16[768,4096]{1,0:T(8,128)(2,1)} %param.9, s32[]{:T(128)S(6)} %select_n.137), kind=kOutput, calls=%fused_computation.25 | convolution fusion | flops 1207959552 | bytes 11403268 | tf_op jit(solution)/shard_map/rd,dkc->rkc/dot_general | solution.py:112
  296.7 19.1 %add_convert_fusion = bf16[768,3,1024]{2,0,1:T(8,128)(2,1)S(1)} fusion(f32[768,3,1024]{2,0,1:T(8,128)} %fusion.22, f32[768,3,1024]{2,0,1:T(8,128)} %fusion.24, f32[768,3,1024]{2,0,1:T(8,128)} %fusion, f32[768,3,1024]{2,0,1:T(8,128)} %fusion.2, f32[768,3,1024]{2,0,1:T(8,128)} %add_add_fusion, f32[768,3,1024]{2,0,1:T(8,128)} %fusion.8, ...), kind=kOutput, calls=%fused_computation | convolution fusion | flops 2432434176 | bytes 65273860 | tf_op jit(solution)/shard_map/while/body/eval_jaxpr/rd,dkc->rkc/dot_general | solution.py:112
  315.8 2.1 copy-done
  318.0 0.1 copy.19
  318.0 2.4 collective-permute-start.11
  320.4 0.2 copy.15
  320.7 0.7 pad_bitcast_fusion.taps
  321.3 0.9 multiply_bitcast_fusion.medium
  322.2 6.7 %copy.14 = bf16[768,3,1024]{0,2,1:T(8,128)(2,1)} copy(bf16[768,3,1024]{2,0,1:T(8,128)(2,1)} %copy-done) | data formatting | bytes 9437184 | tf_op jit(solution)/shard_map/convert_element_type | solution.py:203
  328.9 6.6 %copy.16.own_q.own_k.own_v = bf16[768,3072]{1,0:T(8,128)(2,1)} copy(bf16[768,3072]{0,1:T(8,128)(2,1)} %bitcast.73) | data formatting | bytes 9437184 | tf_op jit(solution)/shard_map/reshape | solution.py:204
  335.5 0.2 collective-permute-done.11.halo_q.halo_k.halo_v
  335.7 0.9 copy-done.1
  336.7 44.6 %shard_map.91 = bf16[768,1024]{1,0:T(8,128)(2,1)} custom-call(bf16[136,3072]{1,0:T(8,128)(2,1)} %copy-done.1, bf16[136,3072]{1,0:T(8,128)(2,1)} %copy-done.1, bf16[136,3072]{1,0:T(8,128)(2,1)} %copy-done.1, bf16[768,3072]{1,0:T(8,128)(2,1)} %copy.16.own_q.own_k.own_v, bf16[768,3072]{1,0:T(8,128)(2,1)} %copy.16.own_q.own_k.own_v, ...), custom_call_target="tpu_custom_call" | custom-call | tf_op jit(solution)/shard_map/pallas_call | solution.py:66
  381.2 1.3 collective-permute-start.13
  382.5 3.5 collective-permute-start.12
  386.0 28.1 %collective-permute-done.13 = bf16[768,1024]{1,0:T(8,128)(2,1)S(1)} collective-permute-done((bf16[768,1024]{1,0:T(8,128)(2,1)}, bf16[768,1024]{1,0:T(8,128)(2,1)S(1)}, u32[]{:S(2)}, u32[]{:S(2)}) %collective-permute-start.13) | collective-permute-done | bytes 1572896 | tf_op jit(solution)/shard_map/ppermute | solution.py:188
  414.1 4.1 collective-permute-start.14
  418.2 3.2 fusion.38
  421.4 3.4 fusion.40
  424.9 3.4 fusion.39
  428.3 4.6 %add_convert_fusion.1 = bf16[768,1024]{1,0:T(8,128)(2,1)} fusion(f32[768,1024]{1,0:T(8,128)S(1)} %fusion.40, f32[768,1024]{1,0:T(8,128)S(1)} %fusion.38, f32[768,1024]{1,0:T(8,128)S(1)} %fusion.39, bf16[768,1024]{1,0:T(8,128)(2,1)S(1)} %collective-permute-done.14, bf16[1024,1024]{1,0:T(8,128)(2,1)} %collective-permute-done.6), kind=kOutput, calls=%fused_computation.2 | convolution fusion | flops 1613758464 | bytes 14680064 | tf_op jit(solution)/shard_map/dot_general | solution.py:192
  (25 shorter events, 0.1 us)
Async XLA Ops:
  0.0 70.2 %collective-permute-start = (bf16[512,3,1024]{2,0,1:T(8,128)(2,1)}, bf16[512,3,1024]{2,0,1:T(8,128)(2,1)}, u32[]{:S(2)}, u32[]{:S(2)}) collective-permute-start(bf16[512,3,1024]{2,0,1:T(8,128)(2,1)} %param.10), channel_id=1, source_target_pairs={{0,8},{8,16},{16,24},{24,28},{28,20},{20,12},{12,4},{4,0},{1,9},{9... | collective-permute-start | bytes 9437192 | tf_op jit(solution)/shard_map/ppermute | solution.py:138
  2.1 69.3 %collective-permute-start.2 = (bf16[512,3,1024]{2,0,1:T(8,128)(2,1)}, bf16[512,3,1024]{2,0,1:T(8,128)(2,1)}, u32[]{:S(2)}, u32[]{:S(2)}) collective-permute-start(bf16[512,3,1024]{2,0,1:T(8,128)(2,1)} %param.10), channel_id=1, source_target_pairs={{0,4},{8,0},{16,8},{24,16},{28,24},{20,28},{12,20},{4,12},{1,5},{9... | collective-permute-start | bytes 9437192 | tf_op jit(solution)/shard_map/ppermute | solution.py:139
  70.2 102.9 %collective-permute-start.1 = (bf16[512,3,1024]{2,0,1:T(8,128)(2,1)}, bf16[512,3,1024]{2,0,1:T(8,128)(2,1)}, u32[]{:S(2)}, u32[]{:S(2)}) collective-permute-start(bf16[512,3,1024]{2,0,1:T(8,128)(2,1)} %collective-permute-done), channel_id=1, source_target_pairs={{0,8},{8,16},{16,24},{24,28},{28,20},{20,12},{12,4},{4,0},{1,9},{9... | collective-permute-start | bytes 9437192 | tf_op jit(solution)/shard_map/ppermute | solution.py:131
  71.4 101.7 %collective-permute-start.3 = (bf16[512,3,1024]{2,0,1:T(8,128)(2,1)}, bf16[512,3,1024]{2,0,1:T(8,128)(2,1)S(1)}, u32[]{:S(2)}, u32[]{:S(2)}) collective-permute-start(bf16[512,3,1024]{2,0,1:T(8,128)(2,1)} %collective-permute-done.2), channel_id=1, source_target_pairs={{0,4},{8,0},{16,8},{24,16},{28,24},{20,28},{12,20},{4,12},{1,5},{9... | collective-permute-start | bytes 9437192 | tf_op jit(solution)/shard_map/ppermute | solution.py:132
  71.7 10.5 %copy-start.7 = (s32[8]{0:T(128)S(1)}, s32[8]{0:T(128)}, u32[]{:S(2)}) copy-start(s32[8]{0:T(128)} %constant.118.clone) | copy-start | bytes 100
  71.7 16.4 %copy-start.5 = (s32[8]{0:T(128)S(1)}, s32[8]{0:T(128)}, u32[]{:S(2)}) copy-start(s32[8]{0:T(128)} %constant.117.clone) | copy-start | bytes 100
  78.8 29.4 %collective-permute-start.4 = (bf16[1024,1024]{1,0:T(8,128)(2,1)}, bf16[1024,1024]{1,0:T(8,128)(2,1)}, u32[]{:S(2)}, u32[]{:S(2)}) collective-permute-start(bf16[1024,1024]{1,0:T(8,128)(2,1)} %get-tuple-element.44), channel_id=1, source_target_pairs={{0,1},{1,0},{2,3},{3,2},{4,5},{5,4},{6,7},{7,6},{8,9},{9,8},{10,11... | collective-permute-start | bytes 6291464 | tf_op jit(solution)/shard_map/ppermute | solution.py:179
  80.5 47.6 %collective-permute-start.5 = (bf16[1024,1024]{1,0:T(8,128)(2,1)}, bf16[1024,1024]{1,0:T(8,128)(2,1)}, u32[]{:S(2)}, u32[]{:S(2)}) collective-permute-start(bf16[1024,1024]{1,0:T(8,128)(2,1)} %get-tuple-element.46), channel_id=1, source_target_pairs={{0,2},{1,3},{2,0},{3,1},{4,6},{5,7},{6,4},{7,5},{8,10},{9,11},{10,... | collective-permute-start | bytes 6291464 | tf_op jit(solution)/shard_map/ppermute | solution.py:179
  82.0 91.2 %collective-permute-start.6 = (bf16[1024,1024]{1,0:T(8,128)(2,1)}, bf16[1024,1024]{1,0:T(8,128)(2,1)}, u32[]{:S(2)}, u32[]{:S(2)}) collective-permute-start(bf16[1024,1024]{1,0:T(8,128)(2,1)} %get-tuple-element.43), channel_id=1, source_target_pairs={{0,3},{1,2},{2,1},{3,0},{4,7},{5,6},{6,5},{7,4},{8,11},{9,10},{10,... | collective-permute-start | bytes 6291464 | tf_op jit(solution)/shard_map/ppermute | solution.py:179
  173.2 69.7 %collective-permute-start.7 = (bf16[512,3,1024]{2,0,1:T(8,128)(2,1)}, bf16[512,3,1024]{2,0,1:T(8,128)(2,1)}, u32[]{:S(2)}, u32[]{:S(2)}) collective-permute-start(bf16[512,3,1024]{2,0,1:T(8,128)(2,1)} %collective-permute-done.1), channel_id=1, source_target_pairs={{0,8},{8,16},{16,24},{24,28},{28,20},{20,12},{12,4},{4,0},{1,9},{9... | collective-permute-start | bytes 9437192 | tf_op jit(solution)/shard_map/while/body/eval_jaxpr/ppermute | solution.py:131
  174.7 79.7 %collective-permute-start.8 = (bf16[512,3,1024]{2,0,1:T(8,128)(2,1)S(1)}, bf16[512,3,1024]{2,0,1:T(8,128)(2,1)}, u32[]{:S(2)}, u32[]{:S(2)}) collective-permute-start(bf16[512,3,1024]{2,0,1:T(8,128)(2,1)S(1)} %collective-permute-done.3), channel_id=1, source_target_pairs={{0,4},{8,0},{16,8},{24,16},{28,24},{20,28},{12,20},{4,12},{1,5},{9... | collective-permute-start | bytes 9437192 | tf_op jit(solution)/shard_map/while/body/eval_jaxpr/ppermute | solution.py:132
  244.4 34.8 %collective-permute-start.9 = (bf16[256,3,1024]{2,0,1:T(8,128)(2,1)S(1)}, bf16[256,3,1024]{2,0,1:T(8,128)(2,1)S(1)}, u32[]{:S(2)}, u32[]{:S(2)}) collective-permute-start(bf16[256,3,1024]{2,0,1:T(8,128)(2,1)S(1)} %slice.16), channel_id=1, source_target_pairs={{0,8},{8,16},{16,24},{24,28},{28,20},{20,12},{12,4},{4,0},{1,9},{9... | collective-permute-start | bytes 4718600 | tf_op jit(solution)/shard_map/ppermute | solution.py:151
  255.9 34.7 %collective-permute-start.10 = (bf16[256,3,1024]{2,0,1:T(8,128)(2,1)S(1)}, bf16[256,3,1024]{2,0,1:T(8,128)(2,1)S(1)}, u32[]{:S(2)}, u32[]{:S(2)}) collective-permute-start(bf16[256,3,1024]{2,0,1:T(8,128)(2,1)S(1)} %slice.17), channel_id=1, source_target_pairs={{0,4},{8,0},{16,8},{24,16},{28,24},{20,28},{12,20},{4,12},{1,5},{9... | collective-permute-start | bytes 4718600 | tf_op jit(solution)/shard_map/ppermute | solution.py:152
  315.8 2.1 copy-start
  317.9 2.5 copy-start.3
  317.9 2.7 copy-start.6
  317.9 2.7 copy-start.4
  318.0 17.7 %collective-permute-start.11 = (bf16[136,3072]{1,0:T(8,128)(2,1)S(1)}, bf16[136,3072]{1,0:T(8,128)(2,1)S(1)}, u32[]{:S(2)}, u32[]{:S(2)}) collective-permute-start(bf16[136,3072]{1,0:T(8,128)(2,1)S(1)} %bitcast.74), channel_id=1, source_target_pairs={{0,4},{4,8},{8,12},{12,16},{16,20},{20,24},{24,28},{1,5},{5,9},{9,... | collective-permute-start | bytes 2506760 | tf_op jit(solution)/shard_map/ppermute | solution.py:205
  335.7 0.9 copy-start.1
  336.7 81.6 %copy-start.2 = (bf16[1024,1024]{1,0:T(8,128)(2,1)S(1)}, bf16[1024,1024]{1,0:T(8,128)(2,1)}, u32[]{:S(2)}) copy-start(bf16[1024,1024]{1,0:T(8,128)(2,1)} %get-tuple-element.39) | copy-start | bytes 6291460
  381.2 32.9 %collective-permute-start.13 = (bf16[768,1024]{1,0:T(8,128)(2,1)}, bf16[768,1024]{1,0:T(8,128)(2,1)S(1)}, u32[]{:S(2)}, u32[]{:S(2)}) collective-permute-start(bf16[768,1024]{1,0:T(8,128)(2,1)} %shard_map.91), channel_id=1, source_target_pairs={{0,2},{1,3},{2,0},{3,1},{4,6},{5,7},{6,4},{7,5},{8,10},{9,11},{10,... | collective-permute-start | bytes 4718600 | tf_op jit(solution)/shard_map/ppermute | solution.py:188
  382.5 42.4 %collective-permute-start.12 = (bf16[768,1024]{1,0:T(8,128)(2,1)}, bf16[768,1024]{1,0:T(8,128)(2,1)S(1)}, u32[]{:S(2)}, u32[]{:S(2)}) collective-permute-start(bf16[768,1024]{1,0:T(8,128)(2,1)} %shard_map.91), channel_id=1, source_target_pairs={{0,1},{1,0},{2,3},{3,2},{4,5},{5,4},{6,7},{7,6},{8,9},{9,8},{10,11... | collective-permute-start | bytes 4718600 | tf_op jit(solution)/shard_map/ppermute | solution.py:188
  414.1 14.1 %collective-permute-start.14 = (bf16[768,1024]{1,0:T(8,128)(2,1)S(1)}, bf16[768,1024]{1,0:T(8,128)(2,1)S(1)}, u32[]{:S(2)}, u32[]{:S(2)}) collective-permute-start(bf16[768,1024]{1,0:T(8,128)(2,1)S(1)} %collective-permute-done.13), channel_id=1, source_target_pairs={{0,1},{1,0},{2,3},{3,2},{4,5},{5,4},{6,7},{7,6},{8,9},{9,8},{10,11... | collective-permute-start | bytes 4718600 | tf_op jit(solution)/shard_map/ppermute | solution.py:188

commit v4 on v3

--- a/solution.py
+++ b/solution.py
@@ -12,20 +12,15 @@
 LANES = 128
 
 
-def filter_kernel(halo_q, halo_k, halo_v, own_q, own_k, own_v, taps, medium, skip, out,
+def filter_kernel(field_q, field_k, field_v, taps, medium, skip, out,
                   raw, prod, shifted, smooth_q):
-    local = own_q.shape[0]
-    ext = HALO + local
+    ext = field_q.shape[0]
+    local = ext - HALO
     taps_count = 7
     short_count = taps.shape[0] // 3
-
-    def load_field(halo_ref, own_ref, slot):
-        raw[slot, 0:HALO, :] = halo_ref[...].astype(jnp.float32)
-        raw[slot, HALO:ext, :] = own_ref[...].astype(jnp.float32)
-
-    load_field(halo_q, own_q, 0)
-    load_field(halo_k, own_k, 1)
-    load_field(halo_v, own_v, 2)
+    raw[0] = field_q[...].astype(jnp.float32)
+    raw[1] = field_k[...].astype(jnp.float32)
+    raw[2] = field_v[...].astype(jnp.float32)
 
     def smooth(slot, first):
         total = jnp.zeros((ext - first, LANES), jnp.float32)
@@ -54,25 +49,22 @@
     lax.fori_loop(0, local // CHUNK, chunk_body, 0)
 
 
-def channel_filter(halo, own, taps, medium, skip):
-    local = own.shape[0]
-    channels = own.shape[1] // 3
+def channel_filter(fields, taps, medium, skip):
+    ext = fields.shape[1]
+    local = ext - HALO
+    channels = fields.shape[2]
     tiles = channels // LANES
-    ext = HALO + local
-
-    def field_spec(rows, field):
-        return pl.BlockSpec((rows, LANES), lambda t: (0, field * tiles + t))
+
+    def field_spec(field):
+        return pl.BlockSpec((None, ext, LANES), lambda t: (field, 0, t))
 
     return pl.pallas_call(
         filter_kernel,
         grid=(tiles,),
         in_specs=[
-            field_spec(HALO, 0),
-            field_spec(HALO, 1),
-            field_spec(HALO, 2),
-            field_spec(local, 0),
-            field_spec(local, 1),
-            field_spec(local, 2),
+            field_spec(0),
+            field_spec(1),
+            field_spec(2),
             pl.BlockSpec((taps.shape[0], LANES), lambda t: (0, t)),
             pl.BlockSpec((medium.shape[0], LANES), lambda t: (0, t)),
             pl.BlockSpec((1, LANES), lambda t: (0, t)),
@@ -85,8 +77,7 @@
             pltpu.VMEM((8, ext, LANES), jnp.float32),
             pltpu.VMEM((local, LANES), jnp.float32),
         ],
-    )(halo, halo, halo, own, own, own, taps, medium, skip)
-
+    )(fields, fields, fields, taps, medium, skip)
 
 def ring_order(count):
     if count % 2:
@@ -109,7 +100,7 @@
 
     def partial(block, source, start, width):
         cols = lax.dynamic_slice_in_dim(tokens, source * rows + start, width, 1)
-        return jnp.einsum("rd,dkc->rkc", cols, block, preferred_element_type=jnp.float32)
+        return jnp.einsum("rd,dkc->krc", cols, block, preferred_element_type=jnp.float32)
 
     total = partial(in_weight, me, 0, rows)
     full_steps = (count - 1) // 2
@@ -199,21 +190,21 @@
     ctx_count = lax.axis_size("ctx")
     medium_count = medium_taps.shape[1]
     short_count = short_taps.shape[2]
-    features, weights = ring_projection(tokens, in_weight, spread_weights(out_weight))
-    features = features.astype(jnp.bfloat16)
-    features = features.reshape(row_count, 3 * channel_count)
-    halo = lax.ppermute(
-        features[row_count - HALO :],
+    earlier = lax.ppermute(
+        tokens[row_count - HALO :],
         "ctx",
         [(k, k + 1) for k in range(ctx_count - 1)],
     )
+    widened = jnp.concatenate([earlier, tokens], axis=0)
+    features, weights = ring_projection(widened, in_weight, spread_weights(out_weight))
+    features = features.astype(jnp.bfloat16)
     lag_values = lax.broadcasted_iota(jnp.float32, (1, medium_count), 1)
     filters = medium_taps * jnp.exp(-medium_decay[:, None] * lag_values)
     taps = jnp.pad(
         jnp.transpose(short_taps, (0, 2, 1)), ((0, 0), (0, 8 - short_count), (0, 0))
     ).reshape(3 * 8, channel_count)
     gated = channel_filter(
-        halo, features, taps, jnp.transpose(filters), skip_gain.reshape(1, channel_count)
+        features, taps, jnp.transpose(filters), skip_gain.reshape(1, channel_count)
     )
     return output_projection(gated, weights).astype(jnp.bfloat16)
 

time: 436 us -> 419 us (0.961)
  waiting for transfers between devices: 237 us -> 208 us
  matrix products: 89.2 us -> 105 us
    ppermute x1, waiting for transfers between devices: 68.1 us -> 0.01 us  [ring_projection(): ahead = lax.ppermute(in_weight, 'ctx', forward)]
    ppermute x1, waiting for transfers between devices: 0.23 us -> 66.2 us  [per_device(): lax.ppermute(tokens[row_count - HALO:], 'ctx', [(k, k + 1) for k in range...]
    ppermute x3, waiting for transfers between devices: 65 us -> 12.3 us  [spread_weights(): weights.append(lax.ppermute(sent, 'tp', pairs))]
    ppermute x2, waiting for transfers between devices: 64.3 us -> 88 us  [ring_step(): moved_ahead = lax.ppermute(ahead, 'ctx', forward)]
    dot_general x9, matrix products: 74.6 us -> 90.9 us  [partial(): jnp.einsum('rd,dkc->krc', cols, block, preferred_element_type=jnp.float32)]
    convert_element_type x1 -> x0, local copies, waits for them, and re-layouts: 6.67 us -> none  [per_device(): features = features.astype(jnp.bfloat16)]
    reshape x1 -> x0, local copies, waits for them, and re-layouts: 6.63 us -> none  [per_device(): features = features.reshape(row_count, 3 * channel_count)]
    concatenate x0 -> x1, local copies, waits for them, and re-layouts: none -> 6.26 us  [per_device(): widened = jnp.concatenate([earlier, tokens], axis=0)]
  transfers between devices with their start and end apart: 15 -> 15, of which waited for: 8 -> 8; matrix products, arithmetic and copies ran while one was open for 20% -> 22% of each run, Pallas kernels for 0% -> 0%
where the time goes in v4:
time: 419 us; the launch traced here: 418 us
  waiting for transfers between devices  208 us (50%)
  matrix products  105 us (25%)
  Pallas kernels  44.3 us (11%)
  local copies, waits for them, and re-layouts  24.4 us (6%)
  starting transfers between devices  24.2 us (6%)
  between operations  10.7 us (3%)
    dot_general x9, matrix products, partial(): jnp.einsum('rd,dkc->krc', cols, block, preferred_element_type=jnp.float32)  90.9 us
    ppermute x2, waiting for transfers between devices, ring_step(): moved_ahead = lax.ppermute(ahead, 'ctx', forward)  88 us
    ppermute x1, waiting for transfers between devices, per_device(): lax.ppermute(tokens[row_count - HALO:], 'ctx', [(k, k + 1) for k in range...  66.2 us
    pallas_call x1, Pallas kernels, channel_filter(): pl.pallas_call(filter_kernel, grid=(tiles,), in_specs=[field_spec(0), fie...  44.3 us
    ppermute x3, waiting for transfers between devices, output_projection(): lax.ppermute(piece, 'tp', pairs)  31.2 us
    dot_general x4, matrix products, output_projection(): jnp.dot(pieces[key], weights[key], preferred_element_type=jnp.float32)  14.6 us
    ppermute x3, waiting for transfers between devices, spread_weights(): weights.append(lax.ppermute(sent, 'tp', pairs))  12.3 us
  transfers between devices with their start and end apart: 15, of which 8 were waited for; matrix products, arithmetic and copies ran while one was open for 22% of the time, Pallas kernels for 0%

profile of v4, /device:TPU:1, one launch (start us, length us, event | category | flops | bytes accessed | tf_op | source)
XLA Modules:
  0.0 418.0 jit_solution(17923784165794926763)
XLA Ops:
  0.0 2.1 collective-permute-start
  2.1 0.0 collective-permute-start.2
  2.1 2.3 slice.9
  4.5 4.3 %collective-permute-start.4 = (bf16[136,4096]{1,0:T(8,128)(2,1)}, bf16[136,4096]{1,0:T(8,128)(2,1)}, u32[]{:S(2)}, u32[]{:S(2)}) collective-permute-start(bf16[136,4096]{1,0:T(8,128)(2,1)} %slice.9), channel_id=1, source_target_pairs={{0,4},{4,8},{8,12},{12,16},{16,20},{20,24},{24,28},{1,5},{5,9},{9,... | collective-permute-start | bytes 3342344 | tf_op jit(solution)/shard_map/ppermute | solution.py:193
  8.8 7.2 %constant_dynamic-slice_fusion = (bf16[1024,1024]{1,0:T(8,128)(2,1)}, bf16[1024,1024]{1,0:T(8,128)(2,1)}, bf16[1024,1024]{1,0:T(8,128)(2,1)}, bf16[1024,1024]{1,0:T(8,128)(2,1)}) fusion(bf16[1024,4096]{1,0:T(8,128)(2,1)} %param.15, s32[]{:T(128)S(6)} %select_n.119, s32[]{:T(128)S(6)} %select_n.117, s32[]{:T(128)S(6)} %select_n.116, s32[]{:T(128)S(6)} %select_n.118), kind=kLoop, calls=%fused_computation.44 | loop fusion | bytes 16777232 | tf_op jit(solution)/shard_map/dynamic_slice | solution.py:169
  16.0 1.5 collective-permute-start.5
  17.5 1.2 collective-permute-start.6
  18.7 0.6 dynamic_slice.71
  24.9 0.7 fusion.35
  26.9 66.2 %collective-permute-done.4 = bf16[136,4096]{1,0:T(8,128)(2,1)} collective-permute-done((bf16[136,4096]{1,0:T(8,128)(2,1)}, bf16[136,4096]{1,0:T(8,128)(2,1)}, u32[]{:S(2)}, u32[]{:S(2)}) %collective-permute-start.4) | collective-permute-done | bytes 1114144 | tf_op jit(solution)/shard_map/ppermute | solution.py:193
  93.1 2.8 collective-permute-start.7
  95.9 2.3 constant_dynamic-update-slice_fusion.1
  98.3 0.0 collective-permute-done
  98.3 3.2 collective-permute-start.1
  101.4 0.0 collective-permute-done.2
  101.4 6.3 %constant_dynamic-update-slice_fusion = bf16[904,4096]{1,0:T(8,128)(2,1)} fusion(bf16[904,4096]{1,0:T(8,128)(2,1)} %constant_dynamic-update-slice_fusion.1, bf16[768,4096]{1,0:T(8,128)(2,1)} %param.9), kind=kLoop, calls=%fused_computation.36 | loop fusion | bytes 12582912 | tf_op jit(solution)/shard_map/concatenate | solution.py:198
  107.7 4.3 %fusion.11 = f32[904,3,1024]{2,0,1:T(8,128)S(1)} fusion(bf16[512,3,1024]{2,0,1:T(8,128)(2,1)S(1)} %copy-done.4, bf16[904,4096]{1,0:T(8,128)(2,1)} %constant_dynamic-update-slice_fusion, s32[]{:T(128)S(6)} %select_n.108), kind=kOutput, calls=%fused_computation.19 | convolution fusion | flops 2843738112 | bytes 15179780 | tf_op jit(solution)/shard_map/rd,dkc->krc/dot_general | solution.py:103
  111.9 9.3 %fusion.9 = f32[904,3,1024]{2,0,1:T(8,128)} fusion(bf16[512,3,1024]{2,0,1:T(8,128)(2,1)} %collective-permute-done, bf16[904,4096]{1,0:T(8,128)(2,1)} %constant_dynamic-update-slice_fusion, s32[]{:T(128)S(6)} %select_n.112), kind=kOutput, calls=%fused_computation.17 | convolution fusion | flops 2843738112 | bytes 15179780 | tf_op jit(solution)/shard_map/rd,dkc->krc/dot_general | solution.py:103
  121.2 9.0 %add_bitcast_fusion = f32[3,904,1024]{2,1,0:T(8,128)} fusion(f32[904,3,1024]{2,0,1:T(8,128)S(1)} %fusion.11, f32[904,3,1024]{2,0,1:T(8,128)} %fusion.9, bf16[512,3,1024]{2,0,1:T(8,128)(2,1)S(1)} %collective-permute-done.2, bf16[904,4096]{1,0:T(8,128)(2,1)} %constant_dynamic-update-slice_fusion, s32[]{:T(128)S(6)} %select_n.115), kind=kOutput, calls=%fused_computation.7 | convolution fusion | flops 2849292288 | bytes 37396484 | tf_op jit(solution)/shard_map/rd,dkc->krc/dot_general | solution.py:103
  130.2 12.3 %collective-permute-done.7 = bf16[1024,1024]{1,0:T(8,128)(2,1)} collective-permute-done((bf16[1024,1024]{1,0:T(8,128)(2,1)}, bf16[1024,1024]{1,0:T(8,128)(2,1)}, u32[]{:S(2)}, u32[]{:S(2)}) %collective-permute-start.7) | collective-permute-done | bytes 2097184 | tf_op jit(solution)/shard_map/ppermute | solution.py:170
  142.5 26.5 %collective-permute-done.1 = bf16[512,3,1024]{2,0,1:T(8,128)(2,1)} collective-permute-done((bf16[512,3,1024]{2,0,1:T(8,128)(2,1)}, bf16[512,3,1024]{2,0,1:T(8,128)(2,1)}, u32[]{:S(2)}, u32[]{:S(2)}) %collective-permute-start.1) | collective-permute-done | bytes 3145760 | tf_op jit(solution)/shard_map/ppermute | solution.py:122
  169.0 2.0 collective-permute-done.3
  171.0 1.3 collective-permute-start.8
  172.3 0.2 collective-permute-start.9
  176.3 1.2 copy.10
  177.6 0.6 pad_bitcast_fusion.taps
  178.2 0.9 multiply_bitcast_fusion.medium
  179.1 61.5 %collective-permute-done.8 = bf16[512,3,1024]{2,0,1:T(8,128)(2,1)} collective-permute-done((bf16[512,3,1024]{2,0,1:T(8,128)(2,1)}, bf16[512,3,1024]{2,0,1:T(8,128)(2,1)}, u32[]{:S(2)}, u32[]{:S(2)}) %collective-permute-start.8) | collective-permute-done | bytes 3145760 | tf_op jit(solution)/shard_map/while/body/eval_jaxpr/ppermute | solution.py:122
  240.6 1.5 slice.12
  242.2 1.5 collective-permute-start.10
  243.7 9.8 %fusion.6 = f32[3,1024,904]{1,2,0:T(8,128)} fusion(bf16[512,3,1024]{2,0,1:T(8,128)(2,1)} %collective-permute-done.1, bf16[904,4096]{1,0:T(8,128)(2,1)} %constant_dynamic-update-slice_fusion, s32[]{:T(128)S(6)} %select_n.122), kind=kOutput, calls=%fused_computation.14 | convolution fusion | flops 2843738112 | bytes 15179780 | tf_op jit(solution)/shard_map/while/body/eval_jaxpr/rd,dkc->krc/dot_general | solution.py:103
  253.5 1.5 slice.13
  255.0 0.2 collective-permute-start.11
  255.2 9.7 %fusion.3 = f32[3,1024,904]{1,2,0:T(8,128)} fusion(bf16[512,3,1024]{2,0,1:T(8,128)(2,1)} %collective-permute-done.8, bf16[904,4096]{1,0:T(8,128)(2,1)} %constant_dynamic-update-slice_fusion, s32[]{:T(128)S(6)} %select_n.128), kind=kOutput, calls=%fused_computation.11 | convolution fusion | flops 2843738112 | bytes 15179780 | tf_op jit(solution)/shard_map/rd,dkc->krc/dot_general | solution.py:103
  264.9 9.6 %fusion.1 = f32[3,1024,904]{1,2,0:T(8,128)} fusion(bf16[512,3,1024]{2,0,1:T(8,128)(2,1)} %collective-permute-done.9, bf16[904,4096]{1,0:T(8,128)(2,1)} %constant_dynamic-update-slice_fusion, s32[]{:T(128)S(6)} %select_n.131), kind=kOutput, calls=%fused_computation.9 | convolution fusion | flops 2843738112 | bytes 15179780 | tf_op jit(solution)/shard_map/rd,dkc->krc/dot_general | solution.py:103
  274.5 2.6 collective-permute-done.10
  277.1 6.8 %fusion.22 = f32[3,1024,904]{1,2,0:T(8,128)} fusion(bf16[256,3,1024]{2,0,1:T(8,128)(2,1)S(1)} %collective-permute-done.10, bf16[904,4096]{1,0:T(8,128)(2,1)} %constant_dynamic-update-slice_fusion, s32[]{:T(128)S(6)} %select_n.134), kind=kOutput, calls=%fused_computation.31 | convolution fusion | flops 1421869056 | bytes 13144068 | tf_op jit(solution)/shard_map/rd,dkc->krc/dot_general | solution.py:103
  283.8 5.6 %collective-permute-done.11 = bf16[256,3,1024]{2,0,1:T(8,128)(2,1)S(1)} collective-permute-done((bf16[256,3,1024]{2,0,1:T(8,128)(2,1)S(1)}, bf16[256,3,1024]{2,0,1:T(8,128)(2,1)S(1)}, u32[]{:S(2)}, u32[]{:S(2)}) %collective-permute-start.11) | collective-permute-done | bytes 1572896 | tf_op jit(solution)/shard_map/ppermute | solution.py:143
  289.4 6.8 %fusion.20 = f32[3,1024,904]{1,2,0:T(8,128)} fusion(bf16[256,3,1024]{2,0,1:T(8,128)(2,1)S(1)} %collective-permute-done.11, bf16[904,4096]{1,0:T(8,128)(2,1)} %constant_dynamic-update-slice_fusion, s32[]{:T(128)S(6)} %select_n.137), kind=kOutput, calls=%fused_computation.29 | convolution fusion | flops 1421869056 | bytes 13144068 | tf_op jit(solution)/shard_map/rd,dkc->krc/dot_general | solution.py:103
  296.2 25.8 %fusion.field_q.field_k.field_v = bf16[3,904,1024]{2,1,0:T(8,128)(2,1)} fusion(f32[3,1024,904]{1,2,0:T(8,128)} %fusion.20, f32[3,1024,904]{1,2,0:T(8,128)} %fusion.22, f32[3,1024,904]{1,2,0:T(8,128)} %fusion.1, f32[3,1024,904]{1,2,0:T(8,128)} %fusion.3, f32[3,904,1024]{2,1,0:T(8,128)} %add_bitcast_fusion, f32[3,1024,904]{1,2,0:T(8,128)} %fusion.6, ...), kind=kOutput, calls=%fused_computation.1 | convolution fusion | flops 2863177728 | bytes 76275712 | tf_op jit(solution)/shard_map/while/body/eval_jaxpr/rd,dkc->krc/dot_general | solution.py:103
  322.0 44.3 %shard_map.91 = bf16[768,1024]{1,0:T(8,128)(2,1)} custom-call(bf16[3,904,1024]{2,1,0:T(8,128)(2,1)} %fusion.field_q.field_k.field_v, bf16[3,904,1024]{2,1,0:T(8,128)(2,1)} %fusion.field_q.field_k.field_v, bf16[3,904,1024]{2,1,0:T(8,128)(2,1)} %fusion.field_q.field_k.field_v, f32[24,1024]{1,0:T(8,128)} %pad_bitcast_fusion.taps, ...), custom_call_target="tpu_custom_call" | custom-call | tf_op jit(solution)/shard_map/pallas_call | solution.py:61
  366.3 2.5 collective-permute-start.12
  368.8 31.2 %collective-permute-done.13 = bf16[768,1024]{1,0:T(8,128)(2,1)S(1)} collective-permute-done((bf16[768,1024]{1,0:T(8,128)(2,1)}, bf16[768,1024]{1,0:T(8,128)(2,1)S(1)}, u32[]{:S(2)}, u32[]{:S(2)}) %collective-permute-start.13) | collective-permute-done | bytes 1572896 | tf_op jit(solution)/shard_map/ppermute | solution.py:179
  400.0 3.4 collective-permute-start.14
  403.4 3.2 fusion.36
  406.6 3.4 fusion.38
  410.0 3.4 fusion.37
  413.4 4.6 %add_convert_fusion = bf16[768,1024]{1,0:T(8,128)(2,1)} fusion(f32[768,1024]{1,0:T(8,128)S(1)} %fusion.38, f32[768,1024]{1,0:T(8,128)S(1)} %fusion.36, f32[768,1024]{1,0:T(8,128)S(1)} %fusion.37, bf16[768,1024]{1,0:T(8,128)(2,1)S(1)} %collective-permute-done.14, bf16[1024,1024]{1,0:T(8,128)(2,1)} %collective-permute-done.7), kind=kOutput, calls=%fused_computation.8 | convolution fusion | flops 1613758464 | bytes 14680064 | tf_op jit(solution)/shard_map/dot_general | solution.py:183
  (20 shorter events, 0.0 us)
Async XLA Ops:
  0.0 98.3 %collective-permute-start = (bf16[512,3,1024]{2,0,1:T(8,128)(2,1)}, bf16[512,3,1024]{2,0,1:T(8,128)(2,1)}, u32[]{:S(2)}, u32[]{:S(2)}) collective-permute-start(bf16[512,3,1024]{2,0,1:T(8,128)(2,1)} %param.10), channel_id=1, source_target_pairs={{0,8},{8,16},{16,24},{24,28},{28,20},{20,12},{12,4},{4,0},{1,9},{9... | collective-permute-start | bytes 9437192 | tf_op jit(solution)/shard_map/ppermute | solution.py:129
  2.1 99.3 %collective-permute-start.2 = (bf16[512,3,1024]{2,0,1:T(8,128)(2,1)}, bf16[512,3,1024]{2,0,1:T(8,128)(2,1)S(1)}, u32[]{:S(2)}, u32[]{:S(2)}) collective-permute-start(bf16[512,3,1024]{2,0,1:T(8,128)(2,1)} %param.10), channel_id=1, source_target_pairs={{0,4},{8,0},{16,8},{24,16},{28,24},{20,28},{12,20},{4,12},{1,5},{9... | collective-permute-start | bytes 9437192 | tf_op jit(solution)/shard_map/ppermute | solution.py:130
  4.5 88.7 %collective-permute-start.4 = (bf16[136,4096]{1,0:T(8,128)(2,1)}, bf16[136,4096]{1,0:T(8,128)(2,1)}, u32[]{:S(2)}, u32[]{:S(2)}) collective-permute-start(bf16[136,4096]{1,0:T(8,128)(2,1)} %slice.9), channel_id=1, source_target_pairs={{0,4},{4,8},{8,12},{12,16},{16,20},{20,24},{24,28},{1,5},{5,9},{9,... | collective-permute-start | bytes 3342344 | tf_op jit(solution)/shard_map/ppermute | solution.py:193
  8.8 9.9 %copy-start.5 = (s32[8]{0:T(128)S(1)}, s32[8]{0:T(128)}, u32[]{:S(2)}) copy-start(s32[8]{0:T(128)} %constant.118.clone) | copy-start | bytes 100
  8.8 16.1 %copy-start.2 = (s32[8]{0:T(128)S(1)}, s32[8]{0:T(128)}, u32[]{:S(2)}) copy-start(s32[8]{0:T(128)} %constant.117.clone) | copy-start | bytes 100
  16.0 114.2 %collective-permute-start.5 = (bf16[1024,1024]{1,0:T(8,128)(2,1)}, bf16[1024,1024]{1,0:T(8,128)(2,1)}, u32[]{:S(2)}, u32[]{:S(2)}) collective-permute-start(bf16[1024,1024]{1,0:T(8,128)(2,1)} %get-tuple-element.44), channel_id=1, source_target_pairs={{0,1},{1,0},{2,3},{3,2},{4,5},{5,4},{6,7},{7,6},{8,9},{9,8},{10,11... | collective-permute-start | bytes 6291464 | tf_op jit(solution)/shard_map/ppermute | solution.py:170
  17.5 112.7 %collective-permute-start.6 = (bf16[1024,1024]{1,0:T(8,128)(2,1)}, bf16[1024,1024]{1,0:T(8,128)(2,1)}, u32[]{:S(2)}, u32[]{:S(2)}) collective-permute-start(bf16[1024,1024]{1,0:T(8,128)(2,1)} %get-tuple-element.46), channel_id=1, source_target_pairs={{0,2},{1,3},{2,0},{3,1},{4,6},{5,7},{6,4},{7,5},{8,10},{9,11},{10,... | collective-permute-start | bytes 6291464 | tf_op jit(solution)/shard_map/ppermute | solution.py:170
  93.1 49.4 %collective-permute-start.7 = (bf16[1024,1024]{1,0:T(8,128)(2,1)}, bf16[1024,1024]{1,0:T(8,128)(2,1)}, u32[]{:S(2)}, u32[]{:S(2)}) collective-permute-start(bf16[1024,1024]{1,0:T(8,128)(2,1)} %get-tuple-element.43), channel_id=1, source_target_pairs={{0,3},{1,2},{2,1},{3,0},{4,7},{5,6},{6,5},{7,4},{8,11},{9,10},{10,... | collective-permute-start | bytes 6291464 | tf_op jit(solution)/shard_map/ppermute | solution.py:170
  98.2 9.4 %copy-start.4 = (bf16[512,3,1024]{2,0,1:T(8,128)(2,1)S(1)}, bf16[512,3,1024]{2,0,1:T(8,128)(2,1)}, u32[]{:S(2)}) copy-start(bf16[512,3,1024]{2,0,1:T(8,128)(2,1)} %param.10) | copy-start | bytes 9437188
  98.3 70.8 %collective-permute-start.1 = (bf16[512,3,1024]{2,0,1:T(8,128)(2,1)}, bf16[512,3,1024]{2,0,1:T(8,128)(2,1)}, u32[]{:S(2)}, u32[]{:S(2)}) collective-permute-start(bf16[512,3,1024]{2,0,1:T(8,128)(2,1)} %collective-permute-done), channel_id=1, source_target_pairs={{0,8},{8,16},{16,24},{24,28},{28,20},{20,12},{12,4},{4,0},{1,9},{9... | collective-permute-start | bytes 9437192 | tf_op jit(solution)/shard_map/ppermute | solution.py:122
  101.4 69.6 %collective-permute-start.3 = (bf16[512,3,1024]{2,0,1:T(8,128)(2,1)S(1)}, bf16[512,3,1024]{2,0,1:T(8,128)(2,1)}, u32[]{:S(2)}, u32[]{:S(2)}) collective-permute-start(bf16[512,3,1024]{2,0,1:T(8,128)(2,1)S(1)} %collective-permute-done.2), channel_id=1, source_target_pairs={{0,4},{8,0},{16,8},{24,16},{28,24},{20,28},{12,20},{4,12},{1,5},{9... | collective-permute-start | bytes 9437192 | tf_op jit(solution)/shard_map/ppermute | solution.py:123
  121.2 56.3 %copy-start.3 = (f32[1024]{0:T(1024)S(1)}, f32[1024]{0:T(1024)}, u32[]{:S(2)}) copy-start(f32[1024]{0:T(1024)} %param.13) | copy-start | bytes 12292
  121.2 56.4 %copy-start.1 = (f32[3,1024,7]{1,2,0:T(8,128)S(1)}, f32[3,1024,7]{1,2,0:T(8,128)}, u32[]{:S(2)}) copy-start(f32[3,1024,7]{1,2,0:T(8,128)} %param.11) | copy-start | bytes 258052
  171.0 69.6 %collective-permute-start.8 = (bf16[512,3,1024]{2,0,1:T(8,128)(2,1)}, bf16[512,3,1024]{2,0,1:T(8,128)(2,1)}, u32[]{:S(2)}, u32[]{:S(2)}) collective-permute-start(bf16[512,3,1024]{2,0,1:T(8,128)(2,1)} %collective-permute-done.1), channel_id=1, source_target_pairs={{0,8},{8,16},{16,24},{24,28},{28,20},{20,12},{12,4},{4,0},{1,9},{9... | collective-permute-start | bytes 9437192 | tf_op jit(solution)/shard_map/while/body/eval_jaxpr/ppermute | solution.py:122
  172.3 81.2 %collective-permute-start.9 = (bf16[512,3,1024]{2,0,1:T(8,128)(2,1)}, bf16[512,3,1024]{2,0,1:T(8,128)(2,1)}, u32[]{:S(2)}, u32[]{:S(2)}) collective-permute-start(bf16[512,3,1024]{2,0,1:T(8,128)(2,1)} %collective-permute-done.3), channel_id=1, source_target_pairs={{0,4},{8,0},{16,8},{24,16},{28,24},{20,28},{12,20},{4,12},{1,5},{9... | collective-permute-start | bytes 9437192 | tf_op jit(solution)/shard_map/while/body/eval_jaxpr/ppermute | solution.py:123
  242.2 34.9 %collective-permute-start.10 = (bf16[256,3,1024]{2,0,1:T(8,128)(2,1)S(1)}, bf16[256,3,1024]{2,0,1:T(8,128)(2,1)S(1)}, u32[]{:S(2)}, u32[]{:S(2)}) collective-permute-start(bf16[256,3,1024]{2,0,1:T(8,128)(2,1)S(1)} %slice.12), channel_id=1, source_target_pairs={{0,8},{8,16},{16,24},{24,28},{28,20},{20,12},{12,4},{4,0},{1,9},{9... | collective-permute-start | bytes 4718600 | tf_op jit(solution)/shard_map/ppermute | solution.py:142
  255.0 34.4 %collective-permute-start.11 = (bf16[256,3,1024]{2,0,1:T(8,128)(2,1)S(1)}, bf16[256,3,1024]{2,0,1:T(8,128)(2,1)S(1)}, u32[]{:S(2)}, u32[]{:S(2)}) collective-permute-start(bf16[256,3,1024]{2,0,1:T(8,128)(2,1)S(1)} %slice.13), channel_id=1, source_target_pairs={{0,4},{8,0},{16,8},{24,16},{28,24},{20,28},{12,20},{4,12},{1,5},{9... | collective-permute-start | bytes 4718600 | tf_op jit(solution)/shard_map/ppermute | solution.py:143
  322.0 81.3 %copy-start = (bf16[1024,1024]{1,0:T(8,128)(2,1)S(1)}, bf16[1024,1024]{1,0:T(8,128)(2,1)}, u32[]{:S(2)}) copy-start(bf16[1024,1024]{1,0:T(8,128)(2,1)} %get-tuple-element.39) | copy-start | bytes 6291460
  366.3 33.7 %collective-permute-start.13 = (bf16[768,1024]{1,0:T(8,128)(2,1)}, bf16[768,1024]{1,0:T(8,128)(2,1)S(1)}, u32[]{:S(2)}, u32[]{:S(2)}) collective-permute-start(bf16[768,1024]{1,0:T(8,128)(2,1)} %shard_map.91), channel_id=1, source_target_pairs={{0,2},{1,3},{2,0},{3,1},{4,6},{5,7},{6,4},{7,5},{8,10},{9,11},{10,... | collective-permute-start | bytes 4718600 | tf_op jit(solution)/shard_map/ppermute | solution.py:179
  366.3 43.6 %collective-permute-start.12 = (bf16[768,1024]{1,0:T(8,128)(2,1)}, bf16[768,1024]{1,0:T(8,128)(2,1)S(1)}, u32[]{:S(2)}, u32[]{:S(2)}) collective-permute-start(bf16[768,1024]{1,0:T(8,128)(2,1)} %shard_map.91), channel_id=1, source_target_pairs={{0,1},{1,0},{2,3},{3,2},{4,5},{5,4},{6,7},{7,6},{8,9},{9,8},{10,11... | collective-permute-start | bytes 4718600 | tf_op jit(solution)/shard_map/ppermute | solution.py:179
  400.0 13.4 %collective-permute-start.14 = (bf16[768,1024]{1,0:T(8,128)(2,1)S(1)}, bf16[768,1024]{1,0:T(8,128)(2,1)S(1)}, u32[]{:S(2)}, u32[]{:S(2)}) collective-permute-start(bf16[768,1024]{1,0:T(8,128)(2,1)S(1)} %collective-permute-done.13), channel_id=1, source_target_pairs={{0,1},{1,0},{2,3},{3,2},{4,5},{5,4},{6,7},{7,6},{8,9},{9,8},{10,11... | collective-permute-start | bytes 4718600 | tf_op jit(solution)/shard_map/ppermute | solution.py:179

commit v5 on v4

--- a/solution.py
+++ b/solution.py
@@ -50,13 +50,13 @@
 
 
 def channel_filter(fields, taps, medium, skip):
-    ext = fields.shape[1]
+    ext = fields[0].shape[0]
     local = ext - HALO
-    channels = fields.shape[2]
+    channels = fields[0].shape[1]
     tiles = channels // LANES
 
     def field_spec(field):
-        return pl.BlockSpec((None, ext, LANES), lambda t: (field, 0, t))
+        return pl.BlockSpec((ext, LANES), lambda t: (0, t))
 
     return pl.pallas_call(
         filter_kernel,
@@ -77,7 +77,7 @@
             pltpu.VMEM((8, ext, LANES), jnp.float32),
             pltpu.VMEM((local, LANES), jnp.float32),
         ],
-    )(fields, fields, fields, taps, medium, skip)
+    )(*fields, taps, medium, skip)
 
 def ring_order(count):
     if count % 2:
@@ -98,9 +98,18 @@
     order_table = jnp.array(order, jnp.int32)
     my_place = jnp.array(place, jnp.int32)[me]
 
+    def product(cols, block):
+        return tuple(
+            jnp.dot(cols, block[:, field, :], preferred_element_type=jnp.float32)
+            for field in range(block.shape[1])
+        )
+
+    def plus(left, right):
+        return tuple(a + b for a, b in zip(left, right))
+
     def partial(block, source, start, width):
         cols = lax.dynamic_slice_in_dim(tokens, source * rows + start, width, 1)
-        return jnp.einsum("rd,dkc->krc", cols, block, preferred_element_type=jnp.float32)
+        return product(cols, block)
 
     total = partial(in_weight, me, 0, rows)
     full_steps = (count - 1) // 2
@@ -114,8 +123,8 @@
 
     def add_pair(total, ahead, behind, step):
         from_behind, from_ahead = sources(step)
-        total = total + partial(ahead, from_behind, 0, rows)
-        return total + partial(behind, from_ahead, 0, rows)
+        total = plus(total, partial(ahead, from_behind, 0, rows))
+        return plus(total, partial(behind, from_ahead, 0, rows))
 
     def ring_step(step, carry):
         ahead, behind, total = carry
@@ -143,8 +152,15 @@
         last_behind = lax.ppermute(behind[half:], "ctx", backward)
         total = add_pair(total, ahead, behind, full_steps)
         from_behind, from_ahead = sources(full_steps + 1)
-        total = total + partial(last_ahead, from_behind, 0, half)
-        total = total + partial(last_behind, from_ahead, half, rows - half)
+        cols = jnp.concatenate(
+            [
+                lax.dynamic_slice_in_dim(tokens, from_behind * rows, half, 1),
+                lax.dynamic_slice_in_dim(tokens, from_ahead * rows + half, rows - half, 1),
+            ],
+            axis=1,
+        )
+        block = jnp.concatenate([last_ahead, last_behind], axis=0)
+        total = plus(total, product(cols, block))
     else:
         total = add_pair(total, ahead, behind, full_steps)
     return total, riders
@@ -195,9 +211,10 @@
         "ctx",
         [(k, k + 1) for k in range(ctx_count - 1)],
     )
+    earlier, in_weight = lax.optimization_barrier((earlier, in_weight))
     widened = jnp.concatenate([earlier, tokens], axis=0)
     features, weights = ring_projection(widened, in_weight, spread_weights(out_weight))
-    features = features.astype(jnp.bfloat16)
+    features = tuple(part.astype(jnp.bfloat16) for part in features)
     lag_values = lax.broadcasted_iota(jnp.float32, (1, medium_count), 1)
     filters = medium_taps * jnp.exp(-medium_decay[:, None] * lag_values)
     taps = jnp.pad(

time: 419 us -> 398 us (0.950)
  waiting for transfers between devices: 208 us -> 191 us
  matrix products: 105 us -> 98.7 us
  starting transfers between devices: 24.2 us -> 29.9 us
    ppermute x1, waiting for transfers between devices: 66.2 us -> 23.1 us  [per_device(): lax.ppermute(tokens[row_count - HALO:], 'ctx', [(k, k + 1) for k in range...]
    ppermute x1, waiting for transfers between devices: 0.01 us -> 42.3 us  [ring_projection(): ahead = lax.ppermute(in_weight, 'ctx', forward)]
    ppermute x3, starting transfers between devices: 5.85 us -> 14 us  [output_projection(): lax.ppermute(piece, 'tp', pairs)]
    ppermute x3, waiting for transfers between devices: 31.2 us -> 23 us  [output_projection(): lax.ppermute(piece, 'tp', pairs)]
    ppermute x2, waiting for transfers between devices: 88 us -> 80.4 us  [ring_step(): moved_ahead = lax.ppermute(ahead, 'ctx', forward)]
    dot_general x9 -> x24, matrix products: 90.9 us -> 84.1 us  [product(): jnp.dot(cols, block[:, field, :], preferred_element_type=jnp.float32)]
  transfers between devices with their start and end apart: 15 -> 15, of which waited for: 8 -> 9; matrix products, arithmetic and copies ran while one was open for 22% -> 21% of each run, Pallas kernels for 0% -> 0%
where the time goes in v5:
time: 398 us; the launch traced here: 397 us
  waiting for transfers between devices  191 us (48%)
  matrix products  98.7 us (25%)
  Pallas kernels  44.3 us (11%)
  starting transfers between devices  29.9 us (8%)
  local copies, waits for them, and re-layouts  23 us (6%)
  between operations  10 us (3%)
    dot_general x24, matrix products, product(): jnp.dot(cols, block[:, field, :], preferred_element_type=jnp.float32)  84.1 us
    ppermute x2, waiting for transfers between devices, ring_step(): moved_ahead = lax.ppermute(ahead, 'ctx', forward)  80.4 us
    pallas_call x1, Pallas kernels, channel_filter(): pl.pallas_call(filter_kernel, grid=(tiles,), in_specs=[field_spec(0), fie...  44.3 us
    ppermute x1, waiting for transfers between devices, ring_projection(): ahead = lax.ppermute(in_weight, 'ctx', forward)  42.3 us
    ppermute x1, waiting for transfers between devices, per_device(): lax.ppermute(tokens[row_count - HALO:], 'ctx', [(k, k + 1) for k in range...  23.1 us
    ppermute x3, waiting for transfers between devices, output_projection(): lax.ppermute(piece, 'tp', pairs)  23 us
    ppermute x3, waiting for transfers between devices, spread_weights(): weights.append(lax.ppermute(sent, 'tp', pairs))  14.6 us
    dot_general x4, matrix products, output_projection(): jnp.dot(pieces[key], weights[key], preferred_element_type=jnp.float32)  14.6 us
  transfers between devices with their start and end apart: 15, of which 9 were waited for; matrix products, arithmetic and copies ran while one was open for 21% of the time, Pallas kernels for 0%

profile of v5, /device:TPU:1, one launch (start us, length us, event | category | flops | bytes accessed | tf_op | source)
XLA Modules:
  0.0 397.3 jit_solution(6746838589985745869)
XLA Ops:
  0.0 1.3 slice.87
  1.3 4.0 %collective-permute-start = (bf16[136,4096]{1,0:T(8,128)(2,1)S(1)}, bf16[136,4096]{1,0:T(8,128)(2,1)S(1)}, u32[]{:S(2)}, u32[]{:S(2)}) collective-permute-start(bf16[136,4096]{1,0:T(8,128)(2,1)S(1)} %slice.87), channel_id=1, source_target_pairs={{0,4},{4,8},{8,12},{12,16},{16,20},{20,24},{24,28},{1,5},{5,9},{9,... | collective-permute-start | bytes 3342344 | tf_op jit(solution)/shard_map/ppermute | solution.py:209
  5.4 23.1 %collective-permute-done = bf16[136,4096]{1,0:T(8,128)(2,1)S(1)} collective-permute-done((bf16[136,4096]{1,0:T(8,128)(2,1)S(1)}, bf16[136,4096]{1,0:T(8,128)(2,1)S(1)}, u32[]{:S(2)}, u32[]{:S(2)}) %collective-permute-start) | collective-permute-done | bytes 1114144 | tf_op jit(solution)/shard_map/ppermute | solution.py:209
  29.5 3.2 collective-permute-start.1
  32.7 7.0 %constant_dynamic-slice_fusion.2 = (bf16[1024,1024]{1,0:T(8,128)(2,1)}, bf16[1024,1024]{1,0:T(8,128)(2,1)}, bf16[1024,1024]{1,0:T(8,128)(2,1)}, bf16[1024,1024]{1,0:T(8,128)(2,1)}) fusion(bf16[1024,4096]{1,0:T(8,128)(2,1)} %param.15, s32[]{:T(128)S(6)} %select_n.119, s32[]{:T(128)S(6)} %select_n.117, s32[]{:T(128)S(6)} %select_n.116, s32[]{:T(128)S(6)} %select_n.118), kind=kLoop, calls=%fused_computation.109 | loop fusion | bytes 16777232 | tf_op jit(solution)/shard_map/dynamic_slice | solution.py:185
  39.7 1.8 collective-permute-start.5
  50.4 1.3 constant_dynamic-update-slice_fusion.1
  51.7 3.4 constant_dynamic-update-slice_fusion
  56.6 42.3 %collective-permute-done.1 = bf16[512,3,1024]{2,0,1:T(8,128)(2,1)} collective-permute-done((bf16[512,3,1024]{2,0,1:T(8,128)(2,1)}, bf16[512,3,1024]{2,0,1:T(8,128)(2,1)}, u32[]{:S(2)}, u32[]{:S(2)}) %collective-permute-start.1) | collective-permute-done | bytes 3145760 | tf_op jit(solution)/shard_map/ppermute | solution.py:138
  98.9 2.1 collective-permute-start.2
  103.4 2.4 fusion.9
  105.7 2.4 fusion.10
  108.1 2.4 fusion.11
  110.5 3.0 add_add_fusion
  113.5 3.1 add_add_fusion.1
  116.7 3.1 add_add_fusion.2
  119.8 14.6 %collective-permute-done.7 = bf16[1024,1024]{1,0:T(8,128)(2,1)} collective-permute-done((bf16[1024,1024]{1,0:T(8,128)(2,1)}, bf16[1024,1024]{1,0:T(8,128)(2,1)}, u32[]{:S(2)}, u32[]{:S(2)}) %collective-permute-start.7) | collective-permute-done | bytes 2097184 | tf_op jit(solution)/shard_map/ppermute | solution.py:186
  134.4 32.0 %collective-permute-done.2 = bf16[512,3,1024]{2,0,1:T(8,128)(2,1)} collective-permute-done((bf16[512,3,1024]{2,0,1:T(8,128)(2,1)}, bf16[512,3,1024]{2,0,1:T(8,128)(2,1)}, u32[]{:S(2)}, u32[]{:S(2)}) %collective-permute-start.2) | collective-permute-done | bytes 3145760 | tf_op jit(solution)/shard_map/ppermute | solution.py:131
  166.4 1.6 collective-permute-done.4
  177.4 2.8 fusion.16
  181.1 2.4 fusion.22
  183.4 2.4 fusion.28
  185.8 48.4 %collective-permute-done.8 = bf16[512,3,1024]{2,0,1:T(8,128)(2,1)} collective-permute-done((bf16[512,3,1024]{2,0,1:T(8,128)(2,1)}, bf16[512,3,1024]{2,0,1:T(8,128)(2,1)}, u32[]{:S(2)}, u32[]{:S(2)}) %collective-permute-start.8) | collective-permute-done | bytes 3145760 | tf_op jit(solution)/shard_map/while/body/eval_jaxpr/ppermute | solution.py:131
  234.2 1.5 slice.122
  235.8 1.3 collective-permute-start.10
  237.1 1.5 slice.123
  238.9 4.2 %fusion.1 = f32[904,1024]{1,0:T(8,128)} fusion(bf16[512,3,1024]{2,0,1:T(8,128)(2,1)} %collective-permute-done.9, bf16[904,4096]{1,0:T(8,128)(2,1)S(1)} %copy-done.4, s32[]{:T(128)S(6)} %select_n.131), kind=kOutput, calls=%fused_computation.10 | convolution fusion | flops 947912704 | bytes 5677060 | tf_op jit(solution)/shard_map/dot_general | solution.py:103
  243.1 4.2 %fusion.4 = f32[904,1024]{1,0:T(8,128)} fusion(bf16[512,3,1024]{2,0,1:T(8,128)(2,1)} %collective-permute-done.9, bf16[904,4096]{1,0:T(8,128)(2,1)S(1)} %copy-done.4, s32[]{:T(128)S(6)} %select_n.131), kind=kOutput, calls=%fused_computation.16 | convolution fusion | flops 947912704 | bytes 5677060 | tf_op jit(solution)/shard_map/dot_general | solution.py:103
  247.3 4.2 %fusion.2 = f32[904,1024]{1,0:T(8,128)} fusion(bf16[512,3,1024]{2,0,1:T(8,128)(2,1)} %collective-permute-done.8, bf16[904,4096]{1,0:T(8,128)(2,1)S(1)} %copy-done.4, s32[]{:T(128)S(6)} %select_n.128), kind=kOutput, calls=%fused_computation.12 | convolution fusion | flops 947912704 | bytes 5677060 | tf_op jit(solution)/shard_map/dot_general | solution.py:103
  251.5 4.3 %fusion.5 = f32[904,1024]{1,0:T(8,128)} fusion(bf16[512,3,1024]{2,0,1:T(8,128)(2,1)} %collective-permute-done.8, bf16[904,4096]{1,0:T(8,128)(2,1)S(1)} %copy-done.4, s32[]{:T(128)S(6)} %select_n.128), kind=kOutput, calls=%fused_computation.18 | convolution fusion | flops 947912704 | bytes 5677060 | tf_op jit(solution)/shard_map/dot_general | solution.py:103
  255.8 4.2 %fusion.8 = f32[904,1024]{1,0:T(8,128)} fusion(bf16[512,3,1024]{2,0,1:T(8,128)(2,1)} %collective-permute-done.8, bf16[904,4096]{1,0:T(8,128)(2,1)S(1)} %copy-done.4, s32[]{:T(128)S(6)} %select_n.128), kind=kOutput, calls=%fused_computation.24 | convolution fusion | flops 947912704 | bytes 5677060 | tf_op jit(solution)/shard_map/dot_general | solution.py:103
  260.0 4.2 %fusion.7 = f32[904,1024]{1,0:T(8,128)} fusion(bf16[512,3,1024]{2,0,1:T(8,128)(2,1)} %collective-permute-done.9, bf16[904,4096]{1,0:T(8,128)(2,1)S(1)} %copy-done.4, s32[]{:T(128)S(6)} %select_n.131), kind=kOutput, calls=%fused_computation.22 | convolution fusion | flops 947912704 | bytes 5677060 | tf_op jit(solution)/shard_map/dot_general | solution.py:103
  264.2 3.0 collective-permute-done.10
  267.2 2.5 collective-permute-done.11
  269.8 3.0 fusion
  272.8 2.9 fusion.3
  275.8 3.0 fusion.6
  278.8 7.8 %add_convert_fusion.field_v = bf16[904,1024]{1,0:T(8,128)(2,1)} fusion(f32[904,1024]{1,0:T(8,128)} %fusion, f32[904,1024]{1,0:T(8,128)} %fusion.1, f32[904,1024]{1,0:T(8,128)} %fusion.2, f32[904,1024]{1,0:T(8,128)S(1)} %copy-done.2, f32[904,1024]{1,0:T(8,128)S(1)} %fusion.16, bf16[512,3,1024]{2,0,1:T(8,128)(2,1)} %collective-permute-done.4, ...), kind=kOutput, calls=%fused_computation | convolution fusion | flops 953466880 | bytes 22339588 | tf_op jit(solution)/shard_map/while/body/eval_jaxpr/dot_general | solution.py:103
  286.6 7.9 %add_convert_fusion.1.field_k = bf16[904,1024]{1,0:T(8,128)(2,1)} fusion(f32[904,1024]{1,0:T(8,128)} %fusion.3, f32[904,1024]{1,0:T(8,128)} %fusion.4, f32[904,1024]{1,0:T(8,128)} %fusion.5, f32[904,1024]{1,0:T(8,128)S(1)} %copy-done.1, f32[904,1024]{1,0:T(8,128)S(1)} %fusion.22, bf16[512,3,1024]{2,0,1:T(8,128)(2,1)} %collective-permute-done.4, ...), kind=kOutput, calls=%fused_computation.1 | convolution fusion | flops 953466880 | bytes 22339588 | tf_op jit(solution)/shard_map/while/body/eval_jaxpr/dot_general | solution.py:103
  294.5 6.9 %add_convert_fusion.2.field_q = bf16[904,1024]{1,0:T(8,128)(2,1)} fusion(f32[904,1024]{1,0:T(8,128)} %fusion.6, f32[904,1024]{1,0:T(8,128)} %fusion.7, f32[904,1024]{1,0:T(8,128)S(1)} %copy-done.5, f32[904,1024]{1,0:T(8,128)S(1)} %copy-done, f32[904,1024]{1,0:T(8,128)S(1)} %fusion.28, bf16[512,3,1024]{2,0,1:T(8,128)(2,1)} %collective-permute-done.4, ...), kind=kOutput, calls=%fused_computation.2 | convolution fusion | flops 953466880 | bytes 22339588 | tf_op jit(solution)/shard_map/while/body/eval_jaxpr/dot_general | solution.py:103
  301.4 44.3 %shard_map.91 = bf16[768,1024]{1,0:T(8,128)(2,1)} custom-call(bf16[904,1024]{1,0:T(8,128)(2,1)} %add_convert_fusion.2.field_q, bf16[904,1024]{1,0:T(8,128)(2,1)} %add_convert_fusion.1.field_k, bf16[904,1024]{1,0:T(8,128)(2,1)} %add_convert_fusion.field_v, f32[24,1024]{1,0:T(8,128)} %pad_bitcast_fusion.taps, f32[128,1024]{1,0:T(8,128)} %multiply_bitcast_fusion.medium, ...), custom_call_target="tpu_custom_call" | custom-call | tf_op jit(solution)/shard_map/pallas_call | solution.py:61
  346.9 6.1 %collective-permute-start.12 = (bf16[768,1024]{1,0:T(8,128)(2,1)}, bf16[768,1024]{1,0:T(8,128)(2,1)S(1)}, u32[]{:S(2)}, u32[]{:S(2)}) collective-permute-start(bf16[768,1024]{1,0:T(8,128)(2,1)} %shard_map.91), channel_id=1, source_target_pairs={{0,1},{1,0},{2,3},{3,2},{4,5},{5,4},{6,7},{7,6},{8,9},{9,8},{10,11... | collective-permute-start | bytes 4718600 | tf_op jit(solution)/shard_map/ppermute | solution.py:195
  353.0 23.0 %collective-permute-done.13 = bf16[768,1024]{1,0:T(8,128)(2,1)S(1)} collective-permute-done((bf16[768,1024]{1,0:T(8,128)(2,1)}, bf16[768,1024]{1,0:T(8,128)(2,1)S(1)}, u32[]{:S(2)}, u32[]{:S(2)}) %collective-permute-start.13) | collective-permute-done | bytes 1572896 | tf_op jit(solution)/shard_map/ppermute | solution.py:195
  376.0 6.7 %collective-permute-start.14 = (bf16[768,1024]{1,0:T(8,128)(2,1)S(1)}, bf16[768,1024]{1,0:T(8,128)(2,1)S(1)}, u32[]{:S(2)}, u32[]{:S(2)}) collective-permute-start(bf16[768,1024]{1,0:T(8,128)(2,1)S(1)} %collective-permute-done.13), channel_id=1, source_target_pairs={{0,1},{1,0},{2,3},{3,2},{4,5},{5,4},{6,7},{7,6},{8,9},{9,8},{10,11... | collective-permute-start | bytes 4718600 | tf_op jit(solution)/shard_map/ppermute | solution.py:195
  382.7 3.2 fusion.91
  385.9 3.4 fusion.93
  389.3 3.4 fusion.92
  392.7 4.6 %add_convert_fusion.3 = bf16[768,1024]{1,0:T(8,128)(2,1)} fusion(f32[768,1024]{1,0:T(8,128)S(1)} %fusion.93, f32[768,1024]{1,0:T(8,128)S(1)} %fusion.91, f32[768,1024]{1,0:T(8,128)S(1)} %fusion.92, bf16[768,1024]{1,0:T(8,128)(2,1)S(1)} %collective-permute-done.14, bf16[1024,1024]{1,0:T(8,128)(2,1)} %collective-permute-done.7), kind=kOutput, calls=%fused_computation.6 | convolution fusion | flops 1613758464 | bytes 14680064 | tf_op jit(solution)/shard_map/dot_general | solution.py:199
  (52 shorter events, 15.8 us)
Async XLA Ops:
  1.3 27.2 %collective-permute-start = (bf16[136,4096]{1,0:T(8,128)(2,1)S(1)}, bf16[136,4096]{1,0:T(8,128)(2,1)S(1)}, u32[]{:S(2)}, u32[]{:S(2)}) collective-permute-start(bf16[136,4096]{1,0:T(8,128)(2,1)S(1)} %slice.87), channel_id=1, source_target_pairs={{0,4},{4,8},{8,12},{12,16},{16,20},{20,24},{24,28},{1,5},{5,9},{9,... | collective-permute-start | bytes 3342344 | tf_op jit(solution)/shard_map/ppermute | solution.py:209
  28.5 1.0 copy-start.7
  29.5 69.4 %collective-permute-start.1 = (bf16[512,3,1024]{2,0,1:T(8,128)(2,1)}, bf16[512,3,1024]{2,0,1:T(8,128)(2,1)}, u32[]{:S(2)}, u32[]{:S(2)}) collective-permute-start(bf16[512,3,1024]{2,0,1:T(8,128)(2,1)} %param.10), channel_id=1, source_target_pairs={{0,8},{8,16},{16,24},{24,28},{28,20},{20,12},{12,4},{4,0},{1,9},{9... | collective-permute-start | bytes 9437192 | tf_op jit(solution)/shard_map/ppermute | solution.py:138
  32.7 68.4 %collective-permute-start.3 = (bf16[512,3,1024]{2,0,1:T(8,128)(2,1)}, bf16[512,3,1024]{2,0,1:T(8,128)(2,1)S(1)}, u32[]{:S(2)}, u32[]{:S(2)}) collective-permute-start(bf16[512,3,1024]{2,0,1:T(8,128)(2,1)} %param.10), channel_id=1, source_target_pairs={{0,4},{8,0},{16,8},{24,16},{28,24},{20,28},{12,20},{4,12},{1,5},{9... | collective-permute-start | bytes 9437192 | tf_op jit(solution)/shard_map/ppermute | solution.py:139
  32.7 10.5 %copy-start.12 = (s32[8]{0:T(128)S(1)}, s32[8]{0:T(128)}, u32[]{:S(2)}) copy-start(s32[8]{0:T(128)} %constant.118.clone) | copy-start | bytes 100
  32.7 15.7 %copy-start.9 = (s32[8]{0:T(128)S(1)}, s32[8]{0:T(128)}, u32[]{:S(2)}) copy-start(s32[8]{0:T(128)} %constant.117.clone) | copy-start | bytes 100
  39.7 80.1 %collective-permute-start.5 = (bf16[1024,1024]{1,0:T(8,128)(2,1)}, bf16[1024,1024]{1,0:T(8,128)(2,1)}, u32[]{:S(2)}, u32[]{:S(2)}) collective-permute-start(bf16[1024,1024]{1,0:T(8,128)(2,1)} %get-tuple-element.58), channel_id=1, source_target_pairs={{0,1},{1,0},{2,3},{3,2},{4,5},{5,4},{6,7},{7,6},{8,9},{9,8},{10,11... | collective-permute-start | bytes 6291464 | tf_op jit(solution)/shard_map/ppermute | solution.py:186
  41.5 78.3 %collective-permute-start.6 = (bf16[1024,1024]{1,0:T(8,128)(2,1)}, bf16[1024,1024]{1,0:T(8,128)(2,1)}, u32[]{:S(2)}, u32[]{:S(2)}) collective-permute-start(bf16[1024,1024]{1,0:T(8,128)(2,1)} %get-tuple-element.60), channel_id=1, source_target_pairs={{0,2},{1,3},{2,0},{3,1},{4,6},{5,7},{6,4},{7,5},{8,10},{9,11},{10,... | collective-permute-start | bytes 6291464 | tf_op jit(solution)/shard_map/ppermute | solution.py:186
  42.7 91.7 %collective-permute-start.7 = (bf16[1024,1024]{1,0:T(8,128)(2,1)}, bf16[1024,1024]{1,0:T(8,128)(2,1)}, u32[]{:S(2)}, u32[]{:S(2)}) collective-permute-start(bf16[1024,1024]{1,0:T(8,128)(2,1)} %get-tuple-element.57), channel_id=1, source_target_pairs={{0,3},{1,2},{2,1},{3,0},{4,7},{5,6},{6,5},{7,4},{8,11},{9,10},{10,... | collective-permute-start | bytes 6291464 | tf_op jit(solution)/shard_map/ppermute | solution.py:186
  51.7 3.7 copy-start.11
  55.4 61.2 %copy-start.3 = (bf16[904,4096]{1,0:T(8,128)(2,1)}, bf16[904,4096]{1,0:T(8,128)(2,1)S(1)}, u32[]{:S(2)}) copy-start(bf16[904,4096]{1,0:T(8,128)(2,1)S(1)} %constant_dynamic-update-slice_fusion) | copy-start | bytes 22216708
  98.9 67.5 %collective-permute-start.2 = (bf16[512,3,1024]{2,0,1:T(8,128)(2,1)}, bf16[512,3,1024]{2,0,1:T(8,128)(2,1)}, u32[]{:S(2)}, u32[]{:S(2)}) collective-permute-start(bf16[512,3,1024]{2,0,1:T(8,128)(2,1)} %collective-permute-done.1), channel_id=1, source_target_pairs={{0,8},{8,16},{16,24},{24,28},{28,20},{20,12},{12,4},{4,0},{1,9},{9... | collective-permute-start | bytes 9437192 | tf_op jit(solution)/shard_map/ppermute | solution.py:131
  101.1 67.0 %collective-permute-start.4 = (bf16[512,3,1024]{2,0,1:T(8,128)(2,1)S(1)}, bf16[512,3,1024]{2,0,1:T(8,128)(2,1)}, u32[]{:S(2)}, u32[]{:S(2)}) collective-permute-start(bf16[512,3,1024]{2,0,1:T(8,128)(2,1)S(1)} %collective-permute-done.3), channel_id=1, source_target_pairs={{0,4},{8,0},{16,8},{24,16},{28,24},{20,28},{12,20},{4,12},{1,5},{9... | collective-permute-start | bytes 9437192 | tf_op jit(solution)/shard_map/ppermute | solution.py:132
  116.7 57.8 %copy-start.10 = (f32[1024]{0:T(1024)S(1)}, f32[1024]{0:T(1024)}, u32[]{:S(2)}) copy-start(f32[1024]{0:T(1024)} %param.13) | copy-start | bytes 12292
  116.7 57.9 %copy-start.8 = (f32[3,1024,7]{1,2,0:T(8,128)S(1)}, f32[3,1024,7]{1,2,0:T(8,128)}, u32[]{:S(2)}) copy-start(f32[3,1024,7]{1,2,0:T(8,128)} %param.11) | copy-start | bytes 258052
  168.0 66.2 %collective-permute-start.8 = (bf16[512,3,1024]{2,0,1:T(8,128)(2,1)}, bf16[512,3,1024]{2,0,1:T(8,128)(2,1)}, u32[]{:S(2)}, u32[]{:S(2)}) collective-permute-start(bf16[512,3,1024]{2,0,1:T(8,128)(2,1)} %collective-permute-done.2), channel_id=1, source_target_pairs={{0,8},{8,16},{16,24},{24,28},{28,20},{20,12},{12,4},{4,0},{1,9},{9... | collective-permute-start | bytes 9437192 | tf_op jit(solution)/shard_map/while/body/eval_jaxpr/ppermute | solution.py:131
  169.3 67.8 %collective-permute-start.9 = (bf16[512,3,1024]{2,0,1:T(8,128)(2,1)}, bf16[512,3,1024]{2,0,1:T(8,128)(2,1)}, u32[]{:S(2)}, u32[]{:S(2)}) collective-permute-start(bf16[512,3,1024]{2,0,1:T(8,128)(2,1)} %collective-permute-done.4), channel_id=1, source_target_pairs={{0,4},{8,0},{16,8},{24,16},{28,24},{20,28},{12,20},{4,12},{1,5},{9... | collective-permute-start | bytes 9437192 | tf_op jit(solution)/shard_map/while/body/eval_jaxpr/ppermute | solution.py:132
  177.4 3.7 copy-start.4
  235.8 31.3 %collective-permute-start.10 = (bf16[256,3,1024]{2,0,1:T(8,128)(2,1)S(1)}, bf16[256,3,1024]{2,0,1:T(8,128)(2,1)S(1)}, u32[]{:S(2)}, u32[]{:S(2)}) collective-permute-start(bf16[256,3,1024]{2,0,1:T(8,128)(2,1)S(1)} %slice.122), channel_id=1, source_target_pairs={{0,8},{8,16},{16,24},{24,28},{28,20},{20,12},{12,4},{4,0},{1,9},{9... | collective-permute-start | bytes 4718600 | tf_op jit(solution)/shard_map/ppermute | solution.py:151
  238.7 31.1 %collective-permute-start.11 = (bf16[256,3,1024]{2,0,1:T(8,128)(2,1)S(1)}, bf16[256,3,1024]{2,0,1:T(8,128)(2,1)S(1)}, u32[]{:S(2)}, u32[]{:S(2)}) collective-permute-start(bf16[256,3,1024]{2,0,1:T(8,128)(2,1)S(1)} %slice.123), channel_id=1, source_target_pairs={{0,4},{8,0},{16,8},{24,16},{28,24},{20,28},{12,20},{4,12},{1,5},{9... | collective-permute-start | bytes 4718600 | tf_op jit(solution)/shard_map/ppermute | solution.py:152
  275.8 3.0 copy-start.2
  278.8 7.8 %copy-start.1 = (f32[904,1024]{1,0:T(8,128)S(1)}, f32[904,1024]{1,0:T(8,128)}, u32[]{:S(2)}) copy-start(f32[904,1024]{1,0:T(8,128)} %add_add_fusion.1) | copy-start | bytes 11108356
  286.6 7.9 %copy-start = (f32[904,1024]{1,0:T(8,128)S(1)}, f32[904,1024]{1,0:T(8,128)}, u32[]{:S(2)}) copy-start(f32[904,1024]{1,0:T(8,128)} %add_add_fusion.2) | copy-start | bytes 11108356
  286.6 7.9 %copy-start.5 = (f32[904,1024]{1,0:T(8,128)S(1)}, f32[904,1024]{1,0:T(8,128)}, u32[]{:S(2)}) copy-start(f32[904,1024]{1,0:T(8,128)} %fusion.8) | copy-start | bytes 11108356
  301.4 81.3 %copy-start.6 = (bf16[1024,1024]{1,0:T(8,128)(2,1)S(1)}, bf16[1024,1024]{1,0:T(8,128)(2,1)}, u32[]{:S(2)}) copy-start(bf16[1024,1024]{1,0:T(8,128)(2,1)} %get-tuple-element.53) | copy-start | bytes 6291460
  345.7 30.3 %collective-permute-start.13 = (bf16[768,1024]{1,0:T(8,128)(2,1)}, bf16[768,1024]{1,0:T(8,128)(2,1)S(1)}, u32[]{:S(2)}, u32[]{:S(2)}) collective-permute-start(bf16[768,1024]{1,0:T(8,128)(2,1)} %shard_map.91), channel_id=1, source_target_pairs={{0,2},{1,3},{2,0},{3,1},{4,6},{5,7},{6,4},{7,5},{8,10},{9,11},{10,... | collective-permute-start | bytes 4718600 | tf_op jit(solution)/shard_map/ppermute | solution.py:195
  346.9 42.4 %collective-permute-start.12 = (bf16[768,1024]{1,0:T(8,128)(2,1)}, bf16[768,1024]{1,0:T(8,128)(2,1)S(1)}, u32[]{:S(2)}, u32[]{:S(2)}) collective-permute-start(bf16[768,1024]{1,0:T(8,128)(2,1)} %shard_map.91), channel_id=1, source_target_pairs={{0,1},{1,0},{2,3},{3,2},{4,5},{5,4},{6,7},{7,6},{8,9},{9,8},{10,11... | collective-permute-start | bytes 4718600 | tf_op jit(solution)/shard_map/ppermute | solution.py:195
  376.0 16.8 %collective-permute-start.14 = (bf16[768,1024]{1,0:T(8,128)(2,1)S(1)}, bf16[768,1024]{1,0:T(8,128)(2,1)S(1)}, u32[]{:S(2)}, u32[]{:S(2)}) collective-permute-start(bf16[768,1024]{1,0:T(8,128)(2,1)S(1)} %collective-permute-done.13), channel_id=1, source_target_pairs={{0,1},{1,0},{2,3},{3,2},{4,5},{5,4},{6,7},{7,6},{8,9},{9,8},{10,11... | collective-permute-start | bytes 4718600 | tf_op jit(solution)/shard_map/ppermute | solution.py:195
